TPU v7x, 512 devices: a whole 4x4x16 slice. The times are simulated.
512 devices in a mesh: section: 8 (over x, core), frames: 4 (over y), space: 16 (over z).
Axes of the slice: x: 4, y: 4, z: 16, core: 2. Of those that a mesh axis runs over, the one named last changes fastest.
Arguments:
- base_frames: bfloat16 [8, 32, 128, 8, 128], P(None, 'frames', 'space'), may hold values from -6 to 6
- section_noise: bfloat16 [8, 8, 32, 128, 8, 128], P('section', None, 'frames', 'space'), may hold values from -6 to 6
- noise_levels: bfloat16 [8], P('section'), may hold values from 0.29882812 to 1
- spatial_kernel: bfloat16 [8, 9, 128, 128], P('section'), may hold values from -0.15625 to 0.15625
- temporal_kernel: bfloat16 [8, 3, 128, 128], P('section'), may hold values from -0.15625 to 0.15625
- output_weight: bfloat16 [8, 128, 128], P('section'), may hold values from -0.5 to 0.5
Outputs:
- denoised: bfloat16 [8, 8, 32, 128, 8, 128], P('section', None, 'frames', 'space')
All inputs are finite; a program needn't handle non-finite values.
Results may differ from a plain program's by a relative error of at most 0.008.
Values may be sent and summed in bfloat16 or wider, within the bound.
No kernel may reach another device: no remote copies, remote signals or barrier semaphores. Data moves between devices by JAX's collectives and lax.ppermute only.
A program may use at most 64 MiB of HBM per device.

v0:
```python
import jax
import jax.numpy as jnp
from jax import lax
from jax.sharding import PartitionSpec as P


def extended(block, sides, width):
    for axis, dim in sides:
        count = lax.axis_size(axis)
        forward = [(i, i + 1) for i in range(count - 1)]
        backward = [(target, source) for source, target in forward]
        low = lax.ppermute(
            lax.slice_in_dim(block, block.shape[dim] - width, None, axis=dim), axis, forward
        )
        high = lax.ppermute(lax.slice_in_dim(block, 0, width, axis=dim), axis, backward)
        block = jnp.concatenate([low, block, high], axis=dim)
    return block


def from_behind(array, axis, by):
    peers = lax.axis_size(axis)
    pairs = [(i, i + by) for i in range(peers) if 0 <= i + by < peers]
    return lax.ppermute(array, axis, pairs)


def denoise(previous, noise_part, noise_scale, spatial, temporal, out_weight):
    noisy = previous.astype(jnp.float32) + noise_scale * noise_part.astype(jnp.float32)
    normalized = (
        noisy * lax.rsqrt(jnp.mean(noisy * noisy, axis=-1, keepdims=True) + 1e-05)
    ).astype(jnp.bfloat16)
    bordered = extended(normalized, (("frames", 1), ("space", 2)), 1)
    bordered = jnp.pad(bordered, ((0, 0), (0, 0), (0, 0), (1, 1), (0, 0)))
    num_videos, num_frames, num_rows, num_cols, channels = previous.shape
    accumulated = jnp.zeros((num_videos * num_frames * num_rows * num_cols, channels), jnp.float32)
    for tap_index in range(9):
        row_offset = tap_index // 3
        col_offset = tap_index % 3
        shifted_view = bordered[
            :,
            1 : 1 + num_frames,
            row_offset : row_offset + num_rows,
            col_offset : col_offset + num_cols,
            :,
        ]
        accumulated = accumulated + jnp.dot(
            shifted_view.reshape(-1, channels),
            spatial[tap_index],
            preferred_element_type=jnp.float32,
        )
    for tap_index in range(3):
        shifted_view = bordered[
            :, tap_index : tap_index + num_frames, 1 : 1 + num_rows, 1 : 1 + num_cols, :
        ]
        accumulated = accumulated + jnp.dot(
            shifted_view.reshape(-1, channels),
            temporal[tap_index],
            preferred_element_type=jnp.float32,
        )
    activated = jax.nn.silu(accumulated).astype(jnp.bfloat16)
    estimate = jnp.dot(activated, out_weight, preferred_element_type=jnp.float32).reshape(
        previous.shape
    )
    return (noisy - noise_scale * estimate).astype(jnp.bfloat16)


def on_device(
    base_frames, section_noise, noise_levels, spatial_kernel, temporal_kernel, output_weight
):
    section_place = lax.axis_index("section")
    section_count = lax.axis_size("section")
    video_count = base_frames.shape[0]
    own_noise = section_noise[0]
    noise_scale = noise_levels[0].astype(jnp.float32)
    spatial = spatial_kernel[0]
    temporal = temporal_kernel[0]
    out_weight = output_weight[0]

    def advance(step_index, carried):
        received, collected = carried
        member = step_index - section_place
        clipped = jnp.clip(member, 0, video_count - 1)
        own_input = lax.dynamic_slice_in_dim(base_frames, clipped, 1, 0)
        incoming = jnp.where(section_place == 0, own_input, received)
        noise_slice = lax.dynamic_slice_in_dim(own_noise, clipped, 1, 0)
        produced = denoise(incoming, noise_slice, noise_scale, spatial, temporal, out_weight)
        earlier = lax.dynamic_slice_in_dim(collected, clipped, 1, 0)
        usable = jnp.logical_and(member >= 0, member < video_count)
        collected = lax.dynamic_update_slice_in_dim(
            collected, jnp.where(usable, produced, earlier), clipped, 0
        )
        received = from_behind(produced, "section", 1)
        return (received, collected)

    starting = (jnp.zeros_like(base_frames[:1]), jnp.zeros_like(base_frames))
    finished = lax.fori_loop(0, section_count + video_count - 1, advance, starting)
    result = finished[1][None]
    return result


def solution(mesh):
    return jax.shard_map(
        on_device,
        mesh=mesh,
        in_specs=(
            P(None, "frames", "space", None, None),
            P("section", None, "frames", "space", None, None),
            P("section"),
            P("section", None, None, None),
            P("section", None, None, None),
            P("section", None, None),
        ),
        out_specs=P("section", None, "frames", "space", None, None),
        check_vma=False,
    )
```

profile of v0, /device:TPU:410, one launch (start us, length us, event | category | flops | bytes accessed | tf_op | source)
XLA Modules:
  0.0 432.9 jit_solution(11669371874738588461)
XLA Ops:
  1.8 430.0 %while.17 = (s32[]{:T(128)}, bf16[1,8,8,8,128]{4,3,2,1,0:T(8,128)(2,1)S(1)}, bf16[8,8,8,8,128]{4,3,2,1,0:T(8,128)(2,1)S(1)}, pred[]{:T(512)}, s32[]{:T(128)}, /*...) while((s32[]{:T(128)}, ...), condition=%wide.region_2.3_spmd, body=%wide.region_0.2_spmd.sunk | while | flops 223398400 | bytes 13724076 | solution.py:95
  8.1 4.2 collective-permute-done.1
  12.4 4.1 collective-permute-start.2
  18.6 4.8 %collective-permute-done.3 = bf16[1,10,1,8,128]{4,3,2,1,0:T(8,128)(2,1)S(1)} collective-permute-done((bf16[1,10,1,8,128]{4,3,2,1,0:T(8,128)(2,1)S(1)}, bf16[1,10,1,8,128]{4,3,2,1,0:T(8,128)(2,1)S(1)}, u32[]{:S(2)}, u32[]{:S(2)}) %collective-permute-start.3) | collective-permute-done | bytes 20512 | tf_op jit(solution)/shard_map/while/body/eval_jaxpr/ppermute | solution.py:12
  28.8 4.4 %collective-permute-done.4 = bf16[1,8,8,8,128]{4,3,2,1,0:T(8,128)(2,1)S(1)} collective-permute-done((bf16[1,8,8,8,128]{4,3,2,1,0:T(8,128)(2,1)S(1)}, bf16[1,8,8,8,128]{4,3,2,1,0:T(8,128)(2,1)S(1)}, u32[]{:S(2)}, u32[]{:S(2)}) %collective-permute-start.4) | collective-permute-done | bytes 131104 | tf_op jit(solution)/shard_map/while/body/eval_jaxpr/ppermute | solution.py:23
  39.2 4.2 collective-permute-done.1
  45.3 3.9 collective-permute-start.3
  57.7 4.4 %collective-permute-done.4 = bf16[1,8,8,8,128]{4,3,2,1,0:T(8,128)(2,1)S(1)} collective-permute-done((bf16[1,8,8,8,128]{4,3,2,1,0:T(8,128)(2,1)S(1)}, bf16[1,8,8,8,128]{4,3,2,1,0:T(8,128)(2,1)S(1)}, u32[]{:S(2)}, u32[]{:S(2)}) %collective-permute-start.4) | collective-permute-done | bytes 131104 | tf_op jit(solution)/shard_map/while/body/eval_jaxpr/ppermute | solution.py:23
  68.0 4.2 collective-permute-done.1
  74.2 3.9 collective-permute-start.3
  86.5 4.4 %collective-permute-done.4 = bf16[1,8,8,8,128]{4,3,2,1,0:T(8,128)(2,1)S(1)} collective-permute-done((bf16[1,8,8,8,128]{4,3,2,1,0:T(8,128)(2,1)S(1)}, bf16[1,8,8,8,128]{4,3,2,1,0:T(8,128)(2,1)S(1)}, u32[]{:S(2)}, u32[]{:S(2)}) %collective-permute-start.4) | collective-permute-done | bytes 131104 | tf_op jit(solution)/shard_map/while/body/eval_jaxpr/ppermute | solution.py:23
  96.5 4.2 collective-permute-done.1
  102.6 3.9 collective-permute-start.3
  115.0 4.4 %collective-permute-done.4 = bf16[1,8,8,8,128]{4,3,2,1,0:T(8,128)(2,1)S(1)} collective-permute-done((bf16[1,8,8,8,128]{4,3,2,1,0:T(8,128)(2,1)S(1)}, bf16[1,8,8,8,128]{4,3,2,1,0:T(8,128)(2,1)S(1)}, u32[]{:S(2)}, u32[]{:S(2)}) %collective-permute-start.4) | collective-permute-done | bytes 131104 | tf_op jit(solution)/shard_map/while/body/eval_jaxpr/ppermute | solution.py:23
  124.9 4.2 collective-permute-done.1
  131.0 3.9 collective-permute-start.3
  143.4 4.4 %collective-permute-done.4 = bf16[1,8,8,8,128]{4,3,2,1,0:T(8,128)(2,1)S(1)} collective-permute-done((bf16[1,8,8,8,128]{4,3,2,1,0:T(8,128)(2,1)S(1)}, bf16[1,8,8,8,128]{4,3,2,1,0:T(8,128)(2,1)S(1)}, u32[]{:S(2)}, u32[]{:S(2)}) %collective-permute-start.4) | collective-permute-done | bytes 131104 | tf_op jit(solution)/shard_map/while/body/eval_jaxpr/ppermute | solution.py:23
  153.3 4.2 collective-permute-done.1
  159.4 3.9 collective-permute-start.3
  163.6 2.8 collective-permute-done.3
  171.8 4.4 %collective-permute-done.4 = bf16[1,8,8,8,128]{4,3,2,1,0:T(8,128)(2,1)S(1)} collective-permute-done((bf16[1,8,8,8,128]{4,3,2,1,0:T(8,128)(2,1)S(1)}, bf16[1,8,8,8,128]{4,3,2,1,0:T(8,128)(2,1)S(1)}, u32[]{:S(2)}, u32[]{:S(2)}) %collective-permute-start.4) | collective-permute-done | bytes 131104 | tf_op jit(solution)/shard_map/while/body/eval_jaxpr/ppermute | solution.py:23
  181.7 4.2 collective-permute-done.1
  187.9 3.9 collective-permute-start.3
  200.2 4.4 %collective-permute-done.4 = bf16[1,8,8,8,128]{4,3,2,1,0:T(8,128)(2,1)S(1)} collective-permute-done((bf16[1,8,8,8,128]{4,3,2,1,0:T(8,128)(2,1)S(1)}, bf16[1,8,8,8,128]{4,3,2,1,0:T(8,128)(2,1)S(1)}, u32[]{:S(2)}, u32[]{:S(2)}) %collective-permute-start.4) | collective-permute-done | bytes 131104 | tf_op jit(solution)/shard_map/while/body/eval_jaxpr/ppermute | solution.py:23
  210.1 4.2 collective-permute-done.1
  216.3 3.9 collective-permute-start.3
  228.6 4.4 %collective-permute-done.4 = bf16[1,8,8,8,128]{4,3,2,1,0:T(8,128)(2,1)S(1)} collective-permute-done((bf16[1,8,8,8,128]{4,3,2,1,0:T(8,128)(2,1)S(1)}, bf16[1,8,8,8,128]{4,3,2,1,0:T(8,128)(2,1)S(1)}, u32[]{:S(2)}, u32[]{:S(2)}) %collective-permute-start.4) | collective-permute-done | bytes 131104 | tf_op jit(solution)/shard_map/while/body/eval_jaxpr/ppermute | solution.py:23
  238.5 4.2 collective-permute-done.1
  244.7 3.9 collective-permute-start.3
  257.1 4.4 %collective-permute-done.4 = bf16[1,8,8,8,128]{4,3,2,1,0:T(8,128)(2,1)S(1)} collective-permute-done((bf16[1,8,8,8,128]{4,3,2,1,0:T(8,128)(2,1)S(1)}, bf16[1,8,8,8,128]{4,3,2,1,0:T(8,128)(2,1)S(1)}, u32[]{:S(2)}, u32[]{:S(2)}) %collective-permute-start.4) | collective-permute-done | bytes 131104 | tf_op jit(solution)/shard_map/while/body/eval_jaxpr/ppermute | solution.py:23
  266.9 4.2 collective-permute-done.1
  273.1 3.9 collective-permute-start.3
  285.5 4.4 %collective-permute-done.4 = bf16[1,8,8,8,128]{4,3,2,1,0:T(8,128)(2,1)S(1)} collective-permute-done((bf16[1,8,8,8,128]{4,3,2,1,0:T(8,128)(2,1)S(1)}, bf16[1,8,8,8,128]{4,3,2,1,0:T(8,128)(2,1)S(1)}, u32[]{:S(2)}, u32[]{:S(2)}) %collective-permute-start.4) | collective-permute-done | bytes 131104 | tf_op jit(solution)/shard_map/while/body/eval_jaxpr/ppermute | solution.py:23
  295.4 4.2 collective-permute-done.1
  301.5 3.9 collective-permute-start.3
  313.9 4.4 %collective-permute-done.4 = bf16[1,8,8,8,128]{4,3,2,1,0:T(8,128)(2,1)S(1)} collective-permute-done((bf16[1,8,8,8,128]{4,3,2,1,0:T(8,128)(2,1)S(1)}, bf16[1,8,8,8,128]{4,3,2,1,0:T(8,128)(2,1)S(1)}, u32[]{:S(2)}, u32[]{:S(2)}) %collective-permute-start.4) | collective-permute-done | bytes 131104 | tf_op jit(solution)/shard_map/while/body/eval_jaxpr/ppermute | solution.py:23
  323.8 4.2 collective-permute-done.1
  329.9 3.9 collective-permute-start.3
  342.3 4.4 %collective-permute-done.4 = bf16[1,8,8,8,128]{4,3,2,1,0:T(8,128)(2,1)S(1)} collective-permute-done((bf16[1,8,8,8,128]{4,3,2,1,0:T(8,128)(2,1)S(1)}, bf16[1,8,8,8,128]{4,3,2,1,0:T(8,128)(2,1)S(1)}, u32[]{:S(2)}, u32[]{:S(2)}) %collective-permute-start.4) | collective-permute-done | bytes 131104 | tf_op jit(solution)/shard_map/while/body/eval_jaxpr/ppermute | solution.py:23
  352.2 4.2 collective-permute-done.1
  358.3 3.9 collective-permute-start.3
  370.7 4.4 %collective-permute-done.4 = bf16[1,8,8,8,128]{4,3,2,1,0:T(8,128)(2,1)S(1)} collective-permute-done((bf16[1,8,8,8,128]{4,3,2,1,0:T(8,128)(2,1)S(1)}, bf16[1,8,8,8,128]{4,3,2,1,0:T(8,128)(2,1)S(1)}, u32[]{:S(2)}, u32[]{:S(2)}) %collective-permute-start.4) | collective-permute-done | bytes 131104 | tf_op jit(solution)/shard_map/while/body/eval_jaxpr/ppermute | solution.py:23
  380.6 4.2 collective-permute-done.1
  386.8 3.9 collective-permute-start.3
  399.1 4.4 %collective-permute-done.4 = bf16[1,8,8,8,128]{4,3,2,1,0:T(8,128)(2,1)S(1)} collective-permute-done((bf16[1,8,8,8,128]{4,3,2,1,0:T(8,128)(2,1)S(1)}, bf16[1,8,8,8,128]{4,3,2,1,0:T(8,128)(2,1)S(1)}, u32[]{:S(2)}, u32[]{:S(2)}) %collective-permute-start.4) | collective-permute-done | bytes 131104 | tf_op jit(solution)/shard_map/while/body/eval_jaxpr/ppermute | solution.py:23
  409.0 4.2 collective-permute-done.1
  415.2 3.9 collective-permute-start.3
  427.5 4.4 %collective-permute-done.4 = bf16[1,8,8,8,128]{4,3,2,1,0:T(8,128)(2,1)S(1)} collective-permute-done((bf16[1,8,8,8,128]{4,3,2,1,0:T(8,128)(2,1)S(1)}, bf16[1,8,8,8,128]{4,3,2,1,0:T(8,128)(2,1)S(1)}, u32[]{:S(2)}, u32[]{:S(2)}) %collective-permute-start.4) | collective-permute-done | bytes 131104 | tf_op jit(solution)/shard_map/while/body/eval_jaxpr/ppermute | solution.py:23
  (428 shorter events, 234.2 us)
Async XLA Ops:
  6.7 5.6 %collective-permute-start.1 = (bf16[1,1,8,8,128]{4,3,2,1,0:T(8,128)(2,1)S(1)}, bf16[1,1,8,8,128]{4,3,2,1,0:T(8,128)(2,1)S(1)}, u32[]{:S(2)}, u32[]{:S(2)}) collective-permute-start(bf16[1,1,8,8,128]{4,3,2,1,0:T(8,128)(2,1)S(1)} %get-tuple-element.382), channel_id=1, source_target_pairs={{0,16},{16,32},{32,48},{1,17},{17,33},{33,49},{2,18},{18,34},{34,5... | collective-permute-start | bytes 49160 | tf_op jit(solution)/shard_map/while/body/eval_jaxpr/ppermute | solution.py:12
  12.4 6.2 %collective-permute-start.2 = (bf16[1,10,1,8,128]{4,3,2,1,0:T(8,128)(2,1)S(1)}, bf16[1,10,1,8,128]{4,3,2,1,0:T(8,128)(2,1)S(1)}, u32[]{:S(2)}, u32[]{:S(2)}) collective-permute-start(bf16[1,10,1,8,128]{4,3,2,1,0:T(8,128)(2,1)S(1)} %get-tuple-element.383), channel_id=1, source_target_pairs={{1,0},{2,1},{3,2},{4,3},{5,4},{6,5},{7,6},{8,7},{9,8},{10,9},{11,1... | collective-permute-start | bytes 61448 | tf_op jit(solution)/shard_map/while/body/eval_jaxpr/ppermute | solution.py:15
  16.5 6.9 %collective-permute-start.3 = (bf16[1,10,1,8,128]{4,3,2,1,0:T(8,128)(2,1)S(1)}, bf16[1,10,1,8,128]{4,3,2,1,0:T(8,128)(2,1)S(1)}, u32[]{:S(2)}, u32[]{:S(2)}) collective-permute-start(bf16[1,10,1,8,128]{4,3,2,1,0:T(8,128)(2,1)S(1)} %get-tuple-element.384), channel_id=1, source_target_pairs={{0,1},{1,2},{2,3},{3,4},{4,5},{5,6},{6,7},{7,8},{8,9},{9,10},{10,1... | collective-permute-start | bytes 61448 | tf_op jit(solution)/shard_map/while/body/eval_jaxpr/ppermute | solution.py:12
  26.9 6.3 %collective-permute-start.4 = (bf16[1,8,8,8,128]{4,3,2,1,0:T(8,128)(2,1)S(1)}, bf16[1,8,8,8,128]{4,3,2,1,0:T(8,128)(2,1)S(1)}, u32[]{:S(2)}, u32[]{:S(2)}) collective-permute-start(bf16[1,8,8,8,128]{4,3,2,1,0:T(8,128)(2,1)S(1)} %get-tuple-element.395), channel_id=1, source_target_pairs={{0,64},{64,128},{128,192},{192,256},{256,320},{320,384},{384,448},... | collective-permute-start | bytes 393224 | tf_op jit(solution)/shard_map/while/body/eval_jaxpr/ppermute | solution.py:23
  37.8 5.6 %collective-permute-start.1 = (bf16[1,1,8,8,128]{4,3,2,1,0:T(8,128)(2,1)S(1)}, bf16[1,1,8,8,128]{4,3,2,1,0:T(8,128)(2,1)S(1)}, u32[]{:S(2)}, u32[]{:S(2)}) collective-permute-start(bf16[1,1,8,8,128]{4,3,2,1,0:T(8,128)(2,1)S(1)} %get-tuple-element.382), channel_id=1, source_target_pairs={{0,16},{16,32},{32,48},{1,17},{17,33},{33,49},{2,18},{18,34},{34,5... | collective-permute-start | bytes 49160 | tf_op jit(solution)/shard_map/while/body/eval_jaxpr/ppermute | solution.py:12
  43.4 6.0 %collective-permute-start.2 = (bf16[1,10,1,8,128]{4,3,2,1,0:T(8,128)(2,1)S(1)}, bf16[1,10,1,8,128]{4,3,2,1,0:T(8,128)(2,1)S(1)}, u32[]{:S(2)}, u32[]{:S(2)}) collective-permute-start(bf16[1,10,1,8,128]{4,3,2,1,0:T(8,128)(2,1)S(1)} %get-tuple-element.383), channel_id=1, source_target_pairs={{1,0},{2,1},{3,2},{4,3},{5,4},{6,5},{7,6},{8,7},{9,8},{10,9},{11,1... | collective-permute-start | bytes 61448 | tf_op jit(solution)/shard_map/while/body/eval_jaxpr/ppermute | solution.py:15
  45.3 6.9 %collective-permute-start.3 = (bf16[1,10,1,8,128]{4,3,2,1,0:T(8,128)(2,1)S(1)}, bf16[1,10,1,8,128]{4,3,2,1,0:T(8,128)(2,1)S(1)}, u32[]{:S(2)}, u32[]{:S(2)}) collective-permute-start(bf16[1,10,1,8,128]{4,3,2,1,0:T(8,128)(2,1)S(1)} %get-tuple-element.384), channel_id=1, source_target_pairs={{0,1},{1,2},{2,3},{3,4},{4,5},{5,6},{6,7},{7,8},{8,9},{9,10},{10,1... | collective-permute-start | bytes 61448 | tf_op jit(solution)/shard_map/while/body/eval_jaxpr/ppermute | solution.py:12
  55.8 6.3 %collective-permute-start.4 = (bf16[1,8,8,8,128]{4,3,2,1,0:T(8,128)(2,1)S(1)}, bf16[1,8,8,8,128]{4,3,2,1,0:T(8,128)(2,1)S(1)}, u32[]{:S(2)}, u32[]{:S(2)}) collective-permute-start(bf16[1,8,8,8,128]{4,3,2,1,0:T(8,128)(2,1)S(1)} %get-tuple-element.395), channel_id=1, source_target_pairs={{0,64},{64,128},{128,192},{192,256},{256,320},{320,384},{384,448},... | collective-permute-start | bytes 393224 | tf_op jit(solution)/shard_map/while/body/eval_jaxpr/ppermute | solution.py:23
  66.6 5.6 %collective-permute-start.1 = (bf16[1,1,8,8,128]{4,3,2,1,0:T(8,128)(2,1)S(1)}, bf16[1,1,8,8,128]{4,3,2,1,0:T(8,128)(2,1)S(1)}, u32[]{:S(2)}, u32[]{:S(2)}) collective-permute-start(bf16[1,1,8,8,128]{4,3,2,1,0:T(8,128)(2,1)S(1)} %get-tuple-element.382), channel_id=1, source_target_pairs={{0,16},{16,32},{32,48},{1,17},{17,33},{33,49},{2,18},{18,34},{34,5... | collective-permute-start | bytes 49160 | tf_op jit(solution)/shard_map/while/body/eval_jaxpr/ppermute | solution.py:12
  72.3 6.0 %collective-permute-start.2 = (bf16[1,10,1,8,128]{4,3,2,1,0:T(8,128)(2,1)S(1)}, bf16[1,10,1,8,128]{4,3,2,1,0:T(8,128)(2,1)S(1)}, u32[]{:S(2)}, u32[]{:S(2)}) collective-permute-start(bf16[1,10,1,8,128]{4,3,2,1,0:T(8,128)(2,1)S(1)} %get-tuple-element.383), channel_id=1, source_target_pairs={{1,0},{2,1},{3,2},{4,3},{5,4},{6,5},{7,6},{8,7},{9,8},{10,9},{11,1... | collective-permute-start | bytes 61448 | tf_op jit(solution)/shard_map/while/body/eval_jaxpr/ppermute | solution.py:15
  74.2 6.9 %collective-permute-start.3 = (bf16[1,10,1,8,128]{4,3,2,1,0:T(8,128)(2,1)S(1)}, bf16[1,10,1,8,128]{4,3,2,1,0:T(8,128)(2,1)S(1)}, u32[]{:S(2)}, u32[]{:S(2)}) collective-permute-start(bf16[1,10,1,8,128]{4,3,2,1,0:T(8,128)(2,1)S(1)} %get-tuple-element.384), channel_id=1, source_target_pairs={{0,1},{1,2},{2,3},{3,4},{4,5},{5,6},{6,7},{7,8},{8,9},{9,10},{10,1... | collective-permute-start | bytes 61448 | tf_op jit(solution)/shard_map/while/body/eval_jaxpr/ppermute | solution.py:12
  84.6 6.3 %collective-permute-start.4 = (bf16[1,8,8,8,128]{4,3,2,1,0:T(8,128)(2,1)S(1)}, bf16[1,8,8,8,128]{4,3,2,1,0:T(8,128)(2,1)S(1)}, u32[]{:S(2)}, u32[]{:S(2)}) collective-permute-start(bf16[1,8,8,8,128]{4,3,2,1,0:T(8,128)(2,1)S(1)} %get-tuple-element.395), channel_id=1, source_target_pairs={{0,64},{64,128},{128,192},{192,256},{256,320},{320,384},{384,448},... | collective-permute-start | bytes 393224 | tf_op jit(solution)/shard_map/while/body/eval_jaxpr/ppermute | solution.py:23
  100.7 6.0 %collective-permute-start.2 = (bf16[1,10,1,8,128]{4,3,2,1,0:T(8,128)(2,1)S(1)}, bf16[1,10,1,8,128]{4,3,2,1,0:T(8,128)(2,1)S(1)}, u32[]{:S(2)}, u32[]{:S(2)}) collective-permute-start(bf16[1,10,1,8,128]{4,3,2,1,0:T(8,128)(2,1)S(1)} %get-tuple-element.383), channel_id=1, source_target_pairs={{1,0},{2,1},{3,2},{4,3},{5,4},{6,5},{7,6},{8,7},{9,8},{10,9},{11,1... | collective-permute-start | bytes 61448 | tf_op jit(solution)/shard_map/while/body/eval_jaxpr/ppermute | solution.py:15
  102.6 6.9 %collective-permute-start.3 = (bf16[1,10,1,8,128]{4,3,2,1,0:T(8,128)(2,1)S(1)}, bf16[1,10,1,8,128]{4,3,2,1,0:T(8,128)(2,1)S(1)}, u32[]{:S(2)}, u32[]{:S(2)}) collective-permute-start(bf16[1,10,1,8,128]{4,3,2,1,0:T(8,128)(2,1)S(1)} %get-tuple-element.384), channel_id=1, source_target_pairs={{0,1},{1,2},{2,3},{3,4},{4,5},{5,6},{6,7},{7,8},{8,9},{9,10},{10,1... | collective-permute-start | bytes 61448 | tf_op jit(solution)/shard_map/while/body/eval_jaxpr/ppermute | solution.py:12
  113.0 6.3 %collective-permute-start.4 = (bf16[1,8,8,8,128]{4,3,2,1,0:T(8,128)(2,1)S(1)}, bf16[1,8,8,8,128]{4,3,2,1,0:T(8,128)(2,1)S(1)}, u32[]{:S(2)}, u32[]{:S(2)}) collective-permute-start(bf16[1,8,8,8,128]{4,3,2,1,0:T(8,128)(2,1)S(1)} %get-tuple-element.395), channel_id=1, source_target_pairs={{0,64},{64,128},{128,192},{192,256},{256,320},{320,384},{384,448},... | collective-permute-start | bytes 393224 | tf_op jit(solution)/shard_map/while/body/eval_jaxpr/ppermute | solution.py:23
  129.1 6.0 %collective-permute-start.2 = (bf16[1,10,1,8,128]{4,3,2,1,0:T(8,128)(2,1)S(1)}, bf16[1,10,1,8,128]{4,3,2,1,0:T(8,128)(2,1)S(1)}, u32[]{:S(2)}, u32[]{:S(2)}) collective-permute-start(bf16[1,10,1,8,128]{4,3,2,1,0:T(8,128)(2,1)S(1)} %get-tuple-element.383), channel_id=1, source_target_pairs={{1,0},{2,1},{3,2},{4,3},{5,4},{6,5},{7,6},{8,7},{9,8},{10,9},{11,1... | collective-permute-start | bytes 61448 | tf_op jit(solution)/shard_map/while/body/eval_jaxpr/ppermute | solution.py:15
  131.0 6.9 %collective-permute-start.3 = (bf16[1,10,1,8,128]{4,3,2,1,0:T(8,128)(2,1)S(1)}, bf16[1,10,1,8,128]{4,3,2,1,0:T(8,128)(2,1)S(1)}, u32[]{:S(2)}, u32[]{:S(2)}) collective-permute-start(bf16[1,10,1,8,128]{4,3,2,1,0:T(8,128)(2,1)S(1)} %get-tuple-element.384), channel_id=1, source_target_pairs={{0,1},{1,2},{2,3},{3,4},{4,5},{5,6},{6,7},{7,8},{8,9},{9,10},{10,1... | collective-permute-start | bytes 61448 | tf_op jit(solution)/shard_map/while/body/eval_jaxpr/ppermute | solution.py:12
  141.5 6.3 %collective-permute-start.4 = (bf16[1,8,8,8,128]{4,3,2,1,0:T(8,128)(2,1)S(1)}, bf16[1,8,8,8,128]{4,3,2,1,0:T(8,128)(2,1)S(1)}, u32[]{:S(2)}, u32[]{:S(2)}) collective-permute-start(bf16[1,8,8,8,128]{4,3,2,1,0:T(8,128)(2,1)S(1)} %get-tuple-element.395), channel_id=1, source_target_pairs={{0,64},{64,128},{128,192},{192,256},{256,320},{320,384},{384,448},... | collective-permute-start | bytes 393224 | tf_op jit(solution)/shard_map/while/body/eval_jaxpr/ppermute | solution.py:23
  157.5 6.0 %collective-permute-start.2 = (bf16[1,10,1,8,128]{4,3,2,1,0:T(8,128)(2,1)S(1)}, bf16[1,10,1,8,128]{4,3,2,1,0:T(8,128)(2,1)S(1)}, u32[]{:S(2)}, u32[]{:S(2)}) collective-permute-start(bf16[1,10,1,8,128]{4,3,2,1,0:T(8,128)(2,1)S(1)} %get-tuple-element.383), channel_id=1, source_target_pairs={{1,0},{2,1},{3,2},{4,3},{5,4},{6,5},{7,6},{8,7},{9,8},{10,9},{11,1... | collective-permute-start | bytes 61448 | tf_op jit(solution)/shard_map/while/body/eval_jaxpr/ppermute | solution.py:15
  159.4 6.9 %collective-permute-start.3 = (bf16[1,10,1,8,128]{4,3,2,1,0:T(8,128)(2,1)S(1)}, bf16[1,10,1,8,128]{4,3,2,1,0:T(8,128)(2,1)S(1)}, u32[]{:S(2)}, u32[]{:S(2)}) collective-permute-start(bf16[1,10,1,8,128]{4,3,2,1,0:T(8,128)(2,1)S(1)} %get-tuple-element.384), channel_id=1, source_target_pairs={{0,1},{1,2},{2,3},{3,4},{4,5},{5,6},{6,7},{7,8},{8,9},{9,10},{10,1... | collective-permute-start | bytes 61448 | tf_op jit(solution)/shard_map/while/body/eval_jaxpr/ppermute | solution.py:12
  169.9 6.3 %collective-permute-start.4 = (bf16[1,8,8,8,128]{4,3,2,1,0:T(8,128)(2,1)S(1)}, bf16[1,8,8,8,128]{4,3,2,1,0:T(8,128)(2,1)S(1)}, u32[]{:S(2)}, u32[]{:S(2)}) collective-permute-start(bf16[1,8,8,8,128]{4,3,2,1,0:T(8,128)(2,1)S(1)} %get-tuple-element.395), channel_id=1, source_target_pairs={{0,64},{64,128},{128,192},{192,256},{256,320},{320,384},{384,448},... | collective-permute-start | bytes 393224 | tf_op jit(solution)/shard_map/while/body/eval_jaxpr/ppermute | solution.py:23
  185.9 6.0 %collective-permute-start.2 = (bf16[1,10,1,8,128]{4,3,2,1,0:T(8,128)(2,1)S(1)}, bf16[1,10,1,8,128]{4,3,2,1,0:T(8,128)(2,1)S(1)}, u32[]{:S(2)}, u32[]{:S(2)}) collective-permute-start(bf16[1,10,1,8,128]{4,3,2,1,0:T(8,128)(2,1)S(1)} %get-tuple-element.383), channel_id=1, source_target_pairs={{1,0},{2,1},{3,2},{4,3},{5,4},{6,5},{7,6},{8,7},{9,8},{10,9},{11,1... | collective-permute-start | bytes 61448 | tf_op jit(solution)/shard_map/while/body/eval_jaxpr/ppermute | solution.py:15
  187.9 6.9 %collective-permute-start.3 = (bf16[1,10,1,8,128]{4,3,2,1,0:T(8,128)(2,1)S(1)}, bf16[1,10,1,8,128]{4,3,2,1,0:T(8,128)(2,1)S(1)}, u32[]{:S(2)}, u32[]{:S(2)}) collective-permute-start(bf16[1,10,1,8,128]{4,3,2,1,0:T(8,128)(2,1)S(1)} %get-tuple-element.384), channel_id=1, source_target_pairs={{0,1},{1,2},{2,3},{3,4},{4,5},{5,6},{6,7},{7,8},{8,9},{9,10},{10,1... | collective-permute-start | bytes 61448 | tf_op jit(solution)/shard_map/while/body/eval_jaxpr/ppermute | solution.py:12
  198.3 6.3 %collective-permute-start.4 = (bf16[1,8,8,8,128]{4,3,2,1,0:T(8,128)(2,1)S(1)}, bf16[1,8,8,8,128]{4,3,2,1,0:T(8,128)(2,1)S(1)}, u32[]{:S(2)}, u32[]{:S(2)}) collective-permute-start(bf16[1,8,8,8,128]{4,3,2,1,0:T(8,128)(2,1)S(1)} %get-tuple-element.395), channel_id=1, source_target_pairs={{0,64},{64,128},{128,192},{192,256},{256,320},{320,384},{384,448},... | collective-permute-start | bytes 393224 | tf_op jit(solution)/shard_map/while/body/eval_jaxpr/ppermute | solution.py:23
  214.3 6.0 %collective-permute-start.2 = (bf16[1,10,1,8,128]{4,3,2,1,0:T(8,128)(2,1)S(1)}, bf16[1,10,1,8,128]{4,3,2,1,0:T(8,128)(2,1)S(1)}, u32[]{:S(2)}, u32[]{:S(2)}) collective-permute-start(bf16[1,10,1,8,128]{4,3,2,1,0:T(8,128)(2,1)S(1)} %get-tuple-element.383), channel_id=1, source_target_pairs={{1,0},{2,1},{3,2},{4,3},{5,4},{6,5},{7,6},{8,7},{9,8},{10,9},{11,1... | collective-permute-start | bytes 61448 | tf_op jit(solution)/shard_map/while/body/eval_jaxpr/ppermute | solution.py:15
  216.3 6.9 %collective-permute-start.3 = (bf16[1,10,1,8,128]{4,3,2,1,0:T(8,128)(2,1)S(1)}, bf16[1,10,1,8,128]{4,3,2,1,0:T(8,128)(2,1)S(1)}, u32[]{:S(2)}, u32[]{:S(2)}) collective-permute-start(bf16[1,10,1,8,128]{4,3,2,1,0:T(8,128)(2,1)S(1)} %get-tuple-element.384), channel_id=1, source_target_pairs={{0,1},{1,2},{2,3},{3,4},{4,5},{5,6},{6,7},{7,8},{8,9},{9,10},{10,1... | collective-permute-start | bytes 61448 | tf_op jit(solution)/shard_map/while/body/eval_jaxpr/ppermute | solution.py:12
  226.7 6.3 %collective-permute-start.4 = (bf16[1,8,8,8,128]{4,3,2,1,0:T(8,128)(2,1)S(1)}, bf16[1,8,8,8,128]{4,3,2,1,0:T(8,128)(2,1)S(1)}, u32[]{:S(2)}, u32[]{:S(2)}) collective-permute-start(bf16[1,8,8,8,128]{4,3,2,1,0:T(8,128)(2,1)S(1)} %get-tuple-element.395), channel_id=1, source_target_pairs={{0,64},{64,128},{128,192},{192,256},{256,320},{320,384},{384,448},... | collective-permute-start | bytes 393224 | tf_op jit(solution)/shard_map/while/body/eval_jaxpr/ppermute | solution.py:23
  242.8 6.0 %collective-permute-start.2 = (bf16[1,10,1,8,128]{4,3,2,1,0:T(8,128)(2,1)S(1)}, bf16[1,10,1,8,128]{4,3,2,1,0:T(8,128)(2,1)S(1)}, u32[]{:S(2)}, u32[]{:S(2)}) collective-permute-start(bf16[1,10,1,8,128]{4,3,2,1,0:T(8,128)(2,1)S(1)} %get-tuple-element.383), channel_id=1, source_target_pairs={{1,0},{2,1},{3,2},{4,3},{5,4},{6,5},{7,6},{8,7},{9,8},{10,9},{11,1... | collective-permute-start | bytes 61448 | tf_op jit(solution)/shard_map/while/body/eval_jaxpr/ppermute | solution.py:15
  244.7 6.9 %collective-permute-start.3 = (bf16[1,10,1,8,128]{4,3,2,1,0:T(8,128)(2,1)S(1)}, bf16[1,10,1,8,128]{4,3,2,1,0:T(8,128)(2,1)S(1)}, u32[]{:S(2)}, u32[]{:S(2)}) collective-permute-start(bf16[1,10,1,8,128]{4,3,2,1,0:T(8,128)(2,1)S(1)} %get-tuple-element.384), channel_id=1, source_target_pairs={{0,1},{1,2},{2,3},{3,4},{4,5},{5,6},{6,7},{7,8},{8,9},{9,10},{10,1... | collective-permute-start | bytes 61448 | tf_op jit(solution)/shard_map/while/body/eval_jaxpr/ppermute | solution.py:12
  255.1 6.3 %collective-permute-start.4 = (bf16[1,8,8,8,128]{4,3,2,1,0:T(8,128)(2,1)S(1)}, bf16[1,8,8,8,128]{4,3,2,1,0:T(8,128)(2,1)S(1)}, u32[]{:S(2)}, u32[]{:S(2)}) collective-permute-start(bf16[1,8,8,8,128]{4,3,2,1,0:T(8,128)(2,1)S(1)} %get-tuple-element.395), channel_id=1, source_target_pairs={{0,64},{64,128},{128,192},{192,256},{256,320},{320,384},{384,448},... | collective-permute-start | bytes 393224 | tf_op jit(solution)/shard_map/while/body/eval_jaxpr/ppermute | solution.py:23
  271.2 6.0 %collective-permute-start.2 = (bf16[1,10,1,8,128]{4,3,2,1,0:T(8,128)(2,1)S(1)}, bf16[1,10,1,8,128]{4,3,2,1,0:T(8,128)(2,1)S(1)}, u32[]{:S(2)}, u32[]{:S(2)}) collective-permute-start(bf16[1,10,1,8,128]{4,3,2,1,0:T(8,128)(2,1)S(1)} %get-tuple-element.383), channel_id=1, source_target_pairs={{1,0},{2,1},{3,2},{4,3},{5,4},{6,5},{7,6},{8,7},{9,8},{10,9},{11,1... | collective-permute-start | bytes 61448 | tf_op jit(solution)/shard_map/while/body/eval_jaxpr/ppermute | solution.py:15
  273.1 6.9 %collective-permute-start.3 = (bf16[1,10,1,8,128]{4,3,2,1,0:T(8,128)(2,1)S(1)}, bf16[1,10,1,8,128]{4,3,2,1,0:T(8,128)(2,1)S(1)}, u32[]{:S(2)}, u32[]{:S(2)}) collective-permute-start(bf16[1,10,1,8,128]{4,3,2,1,0:T(8,128)(2,1)S(1)} %get-tuple-element.384), channel_id=1, source_target_pairs={{0,1},{1,2},{2,3},{3,4},{4,5},{5,6},{6,7},{7,8},{8,9},{9,10},{10,1... | collective-permute-start | bytes 61448 | tf_op jit(solution)/shard_map/while/body/eval_jaxpr/ppermute | solution.py:12
  283.5 6.3 %collective-permute-start.4 = (bf16[1,8,8,8,128]{4,3,2,1,0:T(8,128)(2,1)S(1)}, bf16[1,8,8,8,128]{4,3,2,1,0:T(8,128)(2,1)S(1)}, u32[]{:S(2)}, u32[]{:S(2)}) collective-permute-start(bf16[1,8,8,8,128]{4,3,2,1,0:T(8,128)(2,1)S(1)} %get-tuple-element.395), channel_id=1, source_target_pairs={{0,64},{64,128},{128,192},{192,256},{256,320},{320,384},{384,448},... | collective-permute-start | bytes 393224 | tf_op jit(solution)/shard_map/while/body/eval_jaxpr/ppermute | solution.py:23
  299.6 6.0 %collective-permute-start.2 = (bf16[1,10,1,8,128]{4,3,2,1,0:T(8,128)(2,1)S(1)}, bf16[1,10,1,8,128]{4,3,2,1,0:T(8,128)(2,1)S(1)}, u32[]{:S(2)}, u32[]{:S(2)}) collective-permute-start(bf16[1,10,1,8,128]{4,3,2,1,0:T(8,128)(2,1)S(1)} %get-tuple-element.383), channel_id=1, source_target_pairs={{1,0},{2,1},{3,2},{4,3},{5,4},{6,5},{7,6},{8,7},{9,8},{10,9},{11,1... | collective-permute-start | bytes 61448 | tf_op jit(solution)/shard_map/while/body/eval_jaxpr/ppermute | solution.py:15
  301.5 6.9 %collective-permute-start.3 = (bf16[1,10,1,8,128]{4,3,2,1,0:T(8,128)(2,1)S(1)}, bf16[1,10,1,8,128]{4,3,2,1,0:T(8,128)(2,1)S(1)}, u32[]{:S(2)}, u32[]{:S(2)}) collective-permute-start(bf16[1,10,1,8,128]{4,3,2,1,0:T(8,128)(2,1)S(1)} %get-tuple-element.384), channel_id=1, source_target_pairs={{0,1},{1,2},{2,3},{3,4},{4,5},{5,6},{6,7},{7,8},{8,9},{9,10},{10,1... | collective-permute-start | bytes 61448 | tf_op jit(solution)/shard_map/while/body/eval_jaxpr/ppermute | solution.py:12
  311.9 6.3 %collective-permute-start.4 = (bf16[1,8,8,8,128]{4,3,2,1,0:T(8,128)(2,1)S(1)}, bf16[1,8,8,8,128]{4,3,2,1,0:T(8,128)(2,1)S(1)}, u32[]{:S(2)}, u32[]{:S(2)}) collective-permute-start(bf16[1,8,8,8,128]{4,3,2,1,0:T(8,128)(2,1)S(1)} %get-tuple-element.395), channel_id=1, source_target_pairs={{0,64},{64,128},{128,192},{192,256},{256,320},{320,384},{384,448},... | collective-permute-start | bytes 393224 | tf_op jit(solution)/shard_map/while/body/eval_jaxpr/ppermute | solution.py:23
  328.0 6.0 %collective-permute-start.2 = (bf16[1,10,1,8,128]{4,3,2,1,0:T(8,128)(2,1)S(1)}, bf16[1,10,1,8,128]{4,3,2,1,0:T(8,128)(2,1)S(1)}, u32[]{:S(2)}, u32[]{:S(2)}) collective-permute-start(bf16[1,10,1,8,128]{4,3,2,1,0:T(8,128)(2,1)S(1)} %get-tuple-element.383), channel_id=1, source_target_pairs={{1,0},{2,1},{3,2},{4,3},{5,4},{6,5},{7,6},{8,7},{9,8},{10,9},{11,1... | collective-permute-start | bytes 61448 | tf_op jit(solution)/shard_map/while/body/eval_jaxpr/ppermute | solution.py:15
  329.9 6.9 %collective-permute-start.3 = (bf16[1,10,1,8,128]{4,3,2,1,0:T(8,128)(2,1)S(1)}, bf16[1,10,1,8,128]{4,3,2,1,0:T(8,128)(2,1)S(1)}, u32[]{:S(2)}, u32[]{:S(2)}) collective-permute-start(bf16[1,10,1,8,128]{4,3,2,1,0:T(8,128)(2,1)S(1)} %get-tuple-element.384), channel_id=1, source_target_pairs={{0,1},{1,2},{2,3},{3,4},{4,5},{5,6},{6,7},{7,8},{8,9},{9,10},{10,1... | collective-permute-start | bytes 61448 | tf_op jit(solution)/shard_map/while/body/eval_jaxpr/ppermute | solution.py:12
  340.4 6.3 %collective-permute-start.4 = (bf16[1,8,8,8,128]{4,3,2,1,0:T(8,128)(2,1)S(1)}, bf16[1,8,8,8,128]{4,3,2,1,0:T(8,128)(2,1)S(1)}, u32[]{:S(2)}, u32[]{:S(2)}) collective-permute-start(bf16[1,8,8,8,128]{4,3,2,1,0:T(8,128)(2,1)S(1)} %get-tuple-element.395), channel_id=1, source_target_pairs={{0,64},{64,128},{128,192},{192,256},{256,320},{320,384},{384,448},... | collective-permute-start | bytes 393224 | tf_op jit(solution)/shard_map/while/body/eval_jaxpr/ppermute | solution.py:23
  356.4 6.0 %collective-permute-start.2 = (bf16[1,10,1,8,128]{4,3,2,1,0:T(8,128)(2,1)S(1)}, bf16[1,10,1,8,128]{4,3,2,1,0:T(8,128)(2,1)S(1)}, u32[]{:S(2)}, u32[]{:S(2)}) collective-permute-start(bf16[1,10,1,8,128]{4,3,2,1,0:T(8,128)(2,1)S(1)} %get-tuple-element.383), channel_id=1, source_target_pairs={{1,0},{2,1},{3,2},{4,3},{5,4},{6,5},{7,6},{8,7},{9,8},{10,9},{11,1... | collective-permute-start | bytes 61448 | tf_op jit(solution)/shard_map/while/body/eval_jaxpr/ppermute | solution.py:15
  358.3 6.9 %collective-permute-start.3 = (bf16[1,10,1,8,128]{4,3,2,1,0:T(8,128)(2,1)S(1)}, bf16[1,10,1,8,128]{4,3,2,1,0:T(8,128)(2,1)S(1)}, u32[]{:S(2)}, u32[]{:S(2)}) collective-permute-start(bf16[1,10,1,8,128]{4,3,2,1,0:T(8,128)(2,1)S(1)} %get-tuple-element.384), channel_id=1, source_target_pairs={{0,1},{1,2},{2,3},{3,4},{4,5},{5,6},{6,7},{7,8},{8,9},{9,10},{10,1... | collective-permute-start | bytes 61448 | tf_op jit(solution)/shard_map/while/body/eval_jaxpr/ppermute | solution.py:12
  368.8 6.3 %collective-permute-start.4 = (bf16[1,8,8,8,128]{4,3,2,1,0:T(8,128)(2,1)S(1)}, bf16[1,8,8,8,128]{4,3,2,1,0:T(8,128)(2,1)S(1)}, u32[]{:S(2)}, u32[]{:S(2)}) collective-permute-start(bf16[1,8,8,8,128]{4,3,2,1,0:T(8,128)(2,1)S(1)} %get-tuple-element.395), channel_id=1, source_target_pairs={{0,64},{64,128},{128,192},{192,256},{256,320},{320,384},{384,448},... | collective-permute-start | bytes 393224 | tf_op jit(solution)/shard_map/while/body/eval_jaxpr/ppermute | solution.py:23
  384.8 6.0 %collective-permute-start.2 = (bf16[1,10,1,8,128]{4,3,2,1,0:T(8,128)(2,1)S(1)}, bf16[1,10,1,8,128]{4,3,2,1,0:T(8,128)(2,1)S(1)}, u32[]{:S(2)}, u32[]{:S(2)}) collective-permute-start(bf16[1,10,1,8,128]{4,3,2,1,0:T(8,128)(2,1)S(1)} %get-tuple-element.383), channel_id=1, source_target_pairs={{1,0},{2,1},{3,2},{4,3},{5,4},{6,5},{7,6},{8,7},{9,8},{10,9},{11,1... | collective-permute-start | bytes 61448 | tf_op jit(solution)/shard_map/while/body/eval_jaxpr/ppermute | solution.py:15
  386.8 6.9 %collective-permute-start.3 = (bf16[1,10,1,8,128]{4,3,2,1,0:T(8,128)(2,1)S(1)}, bf16[1,10,1,8,128]{4,3,2,1,0:T(8,128)(2,1)S(1)}, u32[]{:S(2)}, u32[]{:S(2)}) collective-permute-start(bf16[1,10,1,8,128]{4,3,2,1,0:T(8,128)(2,1)S(1)} %get-tuple-element.384), channel_id=1, source_target_pairs={{0,1},{1,2},{2,3},{3,4},{4,5},{5,6},{6,7},{7,8},{8,9},{9,10},{10,1... | collective-permute-start | bytes 61448 | tf_op jit(solution)/shard_map/while/body/eval_jaxpr/ppermute | solution.py:12
  397.2 6.3 %collective-permute-start.4 = (bf16[1,8,8,8,128]{4,3,2,1,0:T(8,128)(2,1)S(1)}, bf16[1,8,8,8,128]{4,3,2,1,0:T(8,128)(2,1)S(1)}, u32[]{:S(2)}, u32[]{:S(2)}) collective-permute-start(bf16[1,8,8,8,128]{4,3,2,1,0:T(8,128)(2,1)S(1)} %get-tuple-element.395), channel_id=1, source_target_pairs={{0,64},{64,128},{128,192},{192,256},{256,320},{320,384},{384,448},... | collective-permute-start | bytes 393224 | tf_op jit(solution)/shard_map/while/body/eval_jaxpr/ppermute | solution.py:23
  413.2 6.0 %collective-permute-start.2 = (bf16[1,10,1,8,128]{4,3,2,1,0:T(8,128)(2,1)S(1)}, bf16[1,10,1,8,128]{4,3,2,1,0:T(8,128)(2,1)S(1)}, u32[]{:S(2)}, u32[]{:S(2)}) collective-permute-start(bf16[1,10,1,8,128]{4,3,2,1,0:T(8,128)(2,1)S(1)} %get-tuple-element.383), channel_id=1, source_target_pairs={{1,0},{2,1},{3,2},{4,3},{5,4},{6,5},{7,6},{8,7},{9,8},{10,9},{11,1... | collective-permute-start | bytes 61448 | tf_op jit(solution)/shard_map/while/body/eval_jaxpr/ppermute | solution.py:15
  415.2 6.9 %collective-permute-start.3 = (bf16[1,10,1,8,128]{4,3,2,1,0:T(8,128)(2,1)S(1)}, bf16[1,10,1,8,128]{4,3,2,1,0:T(8,128)(2,1)S(1)}, u32[]{:S(2)}, u32[]{:S(2)}) collective-permute-start(bf16[1,10,1,8,128]{4,3,2,1,0:T(8,128)(2,1)S(1)} %get-tuple-element.384), channel_id=1, source_target_pairs={{0,1},{1,2},{2,3},{3,4},{4,5},{5,6},{6,7},{7,8},{8,9},{9,10},{10,1... | collective-permute-start | bytes 61448 | tf_op jit(solution)/shard_map/while/body/eval_jaxpr/ppermute | solution.py:12
  425.6 6.3 %collective-permute-start.4 = (bf16[1,8,8,8,128]{4,3,2,1,0:T(8,128)(2,1)S(1)}, bf16[1,8,8,8,128]{4,3,2,1,0:T(8,128)(2,1)S(1)}, u32[]{:S(2)}, u32[]{:S(2)}) collective-permute-start(bf16[1,8,8,8,128]{4,3,2,1,0:T(8,128)(2,1)S(1)} %get-tuple-element.395), channel_id=1, source_target_pairs={{0,64},{64,128},{128,192},{192,256},{256,320},{320,384},{384,448},... | collective-permute-start | bytes 393224 | tf_op jit(solution)/shard_map/while/body/eval_jaxpr/ppermute | solution.py:23
  (31 other events, 123.2 us)
where the time goes:
time: 436 us; the launch traced here: 433 us
  waiting for transfers between devices  174 us (40%)
  starting transfers between devices  166 us (38%)
  other arithmetic  52.2 us (12%)
  matrix products  33 us (8%)
    ppermute x30, waiting for transfers between devices, extended(): lax.ppermute(lax.slice_in_dim(block, block.shape[dim] - width, None, axis...  107 us
    ppermute x30, starting transfers between devices, extended(): lax.ppermute(lax.slice_in_dim(block, block.shape[dim] - width, None, axis...  76.2 us
    ppermute x15, waiting for transfers between devices, from_behind(): return lax.ppermute(array, axis, pairs)  65.3 us
    ppermute x30, starting transfers between devices, extended(): lax.ppermute(lax.slice_in_dim(block, 0, width, axis=dim), axis, backward)  61.4 us
    ppermute x15, starting transfers between devices, from_behind(): return lax.ppermute(array, axis, pairs)  28.8 us
    dot_general x135, matrix products, denoise(): jnp.dot(shifted_view.reshape(-1, channels), spatial[tap_index], preferred...  22.9 us
    reduce_sum x15, other arithmetic, denoise(): jnp.mean(noisy * noisy, axis=-1, keepdims=True) + 1e-05  16.8 us
    convert_element_type x15, other arithmetic, denoise(): normalized = (noisy * lax.rsqrt(jnp.mean(noisy * noisy, axis=-1, keepdims...  15.6 us
  transfers between devices with their start and end apart: 75, of which 60 were waited for; matrix products, arithmetic and copies ran while one was open for 1% of the time, Pallas kernels for 0%

commit v1 on v0

v1 whole, which is shorter than its diff:
```python
import jax
import jax.numpy as jnp
from jax import lax
from jax.sharding import PartitionSpec as P


def shift_in(block, axis, dim):
    count = lax.axis_size(axis)
    forward = [(i, i + 1) for i in range(count - 1)]
    backward = [(i + 1, i) for i in range(count - 1)]
    size = block.shape[dim]
    low = lax.ppermute(lax.slice_in_dim(block, size - 1, size, axis=dim), axis, forward)
    high = lax.ppermute(lax.slice_in_dim(block, 0, 1, axis=dim), axis, backward)
    return low, high


def denoise(previous, noise_part, noise_scale, spatial, temporal, out_weight):
    noisy = previous.astype(jnp.float32) + noise_scale * noise_part.astype(jnp.float32)
    normalized = (
        noisy * lax.rsqrt(jnp.mean(noisy * noisy, axis=-1, keepdims=True) + 1e-05)
    ).astype(jnp.bfloat16)
    low_f, high_f = shift_in(normalized, "frames", 1)
    low_r, high_r = shift_in(normalized, "space", 2)
    rows_ext = jnp.concatenate([low_r, normalized, high_r], axis=2)
    rows_ext = jnp.pad(rows_ext, ((0, 0), (0, 0), (0, 0), (1, 1), (0, 0)))
    frames_ext = jnp.concatenate([low_f, normalized, high_f], axis=1)
    num_videos, num_frames, num_rows, num_cols, channels = previous.shape
    accumulated = jnp.zeros((num_videos * num_frames * num_rows * num_cols, channels), jnp.float32)
    for tap_index in range(9):
        row_offset = tap_index // 3
        col_offset = tap_index % 3
        shifted_view = rows_ext[
            :, :, row_offset : row_offset + num_rows, col_offset : col_offset + num_cols, :
        ]
        accumulated = accumulated + jnp.dot(
            shifted_view.reshape(-1, channels),
            spatial[tap_index],
            preferred_element_type=jnp.float32,
        )
    for tap_index in range(3):
        shifted_view = frames_ext[:, tap_index : tap_index + num_frames]
        accumulated = accumulated + jnp.dot(
            shifted_view.reshape(-1, channels),
            temporal[tap_index],
            preferred_element_type=jnp.float32,
        )
    activated = jax.nn.silu(accumulated).astype(jnp.bfloat16)
    estimate = jnp.dot(activated, out_weight, preferred_element_type=jnp.float32).reshape(
        previous.shape
    )
    return (noisy - noise_scale * estimate).astype(jnp.bfloat16)


def on_device(
    base_frames, section_noise, noise_levels, spatial_kernel, temporal_kernel, output_weight
):
    place = lax.axis_index("section")
    sections = lax.axis_size("section")
    video_count = base_frames.shape[0]
    per_device = video_count // sections
    noise_t = lax.all_to_all(section_noise[0], "section", 0, 0, tiled=True)
    noise_t = noise_t.reshape((sections, per_device) + noise_t.shape[1:])
    levels = lax.all_gather(noise_levels, "section", tiled=True)
    spatial = lax.all_gather(spatial_kernel, "section", tiled=True)
    temporal = lax.all_gather(temporal_kernel, "section", tiled=True)
    out_weight = lax.all_gather(output_weight, "section", tiled=True)
    incoming = lax.dynamic_slice_in_dim(base_frames, place * per_device, per_device, 0)
    results = []
    for k in range(sections):
        incoming = denoise(
            incoming,
            noise_t[k],
            levels[k].astype(jnp.float32),
            spatial[k],
            temporal[k],
            out_weight[k],
        )
        results.append(incoming)
    stacked = jnp.stack(results)
    return lax.all_to_all(stacked, "section", 0, 1, tiled=True)


def solution(mesh):
    return jax.shard_map(
        on_device,
        mesh=mesh,
        in_specs=(
            P(None, "frames", "space", None, None),
            P("section", None, "frames", "space", None, None),
            P("section"),
            P("section", None, None, None),
            P("section", None, None, None),
            P("section", None, None),
        ),
        out_specs=P("section", None, "frames", "space", None, None),
        check_vma=False,
    )
```

time: 436 us -> 241 us (0.55)
  the two profiles are of different devices: /device:TPU:410 before, /device:TPU:384 now
where the time goes in v1:
time: 241 us; the launch traced here: 240 us
  starting transfers between devices  94.4 us (39%)
  blocking collectives  63.5 us (26%)
  waiting for transfers between devices  27.9 us (12%)
  matrix products  22.4 us (9%)
  between operations  20.7 us (9%)
  other arithmetic  6.32 us (3%)
  local copies, waits for them, and re-layouts  4.63 us (2%)
    ppermute x16, starting transfers between devices, shift_in(): high = lax.ppermute(lax.slice_in_dim(block, 0, 1, axis=dim), axis, backward)  50.1 us
    ppermute x16, starting transfers between devices, shift_in(): lax.ppermute(lax.slice_in_dim(block, size - 1, size, axis=dim), axis, for...  39.9 us
    ppermute x16, waiting for transfers between devices, shift_in(): high = lax.ppermute(lax.slice_in_dim(block, 0, 1, axis=dim), axis, backward)  27.2 us
    all_to_all x1, blocking collectives, on_device(): return lax.all_to_all(stacked, 'section', 0, 1, tiled=True)  19.1 us
    unnamed x1, blocking collectives  18.2 us
    dot_general x72, matrix products, denoise(): jnp.dot(shifted_view.reshape(-1, channels), spatial[tap_index], preferred...  15.4 us
    all_gather x1, blocking collectives, on_device(): temporal = lax.all_gather(temporal_kernel, 'section', tiled=True)  13.4 us
    all_gather x1, blocking collectives, on_device(): out_weight = lax.all_gather(output_weight, 'section', tiled=True)  12.8 us
  transfers between devices with their start and end apart: 34, of which 8 were waited for; matrix products, arithmetic and copies ran while one was open for 4% of the time, Pallas kernels for 0%

profile of v1, /device:TPU:384, one launch (start us, length us, event | category | flops | bytes accessed | tf_op | source)
XLA Modules:
  0.0 239.9 jit_solution(10621970173970673217)
XLA Ops:
  7.3 4.3 %all-to-all-start = ((bf16[8,8,8,8,128]{4,3,2,1,0:T(8,128)(2,1)}), bf16[8,8,8,8,128]{4,3,2,1,0:T(8,128)(2,1)S(1)}, u32[]{:S(2)}, u32[]{:S(2)}) async-start(bf16[8,8,8,8,128]{4,3,2,1,0:T(8,128)(2,1)} %bitcast.664), calls=%async_computation | async-start | bytes 2097152 | tf_op jit(solution)/shard_map/all_to_all | solution.py:61
  12.2 1.3 dynamic-slice
  14.3 18.2 %all-reduce.8 = bf16[8]{0:T(256)(128)(2,1)S(1)} all-reduce(bf16[8]{0:T(256)(128)(2,1)S(1)} %dynamic-update-slice), channel_id=1, replica_groups=mesh['section'=8,'frames'=4,'space'=16] {'section'}, use_global_device_ids=true, to_apply=%add.8 | all-reduce | flops 8 | bytes 32
  38.1 12.8 %all_gather.15 = bf16[8,128,128]{2,1,0:T(8,128)(2,1)S(1)} all-gather(bf16[1,128,128]{2,1,0:T(8,128)(2,1)S(1)} %copy-done.4), channel_id=1, replica_groups=mesh['section'=8,'frames'=4,'space'=16] {'section'}, dimensions={0}, use_global_device_ids=true | all-gather | bytes 294912 | tf_op jit(solution)/shard_map/all_gather | solution.py:66
  50.9 13.4 %all_gather.14 = bf16[8,3,128,128]{3,2,1,0:T(8,128)(2,1)S(1)} all-gather(bf16[1,3,128,128]{3,2,1,0:T(8,128)(2,1)S(1)} %copy-done.3), channel_id=1, replica_groups=mesh['section'=8,'frames'=4,'space'=16] {'section'}, dimensions={0}, use_global_device_ids=true | all-gather | bytes 884736 | tf_op jit(solution)/shard_map/all_gather | solution.py:65
  66.4 3.4 %collective-permute-start = (bf16[1,8,1,8,128]{4,3,2,1,0:T(8,128)(2,1)S(1)}, bf16[1,8,1,8,128]{4,3,2,1,0:T(8,128)(2,1)S(1)}, u32[]{:S(2)}, u32[]{:S(2)}) collective-permute-start(bf16[1,8,1,8,128]{4,3,2,1,0:T(8,128)(2,1)S(1)} %get-tuple-element.115), channel_id=1, source_target_pairs={{0,1},{1,2},{2,3},{3,4},{4,5},{5,6},{6,7},{7,8},{8,9},{9,10},{10,1... | collective-permute-start | bytes 49160 | tf_op jit(solution)/shard_map/ppermute | solution.py:12
  69.8 3.7 %collective-permute-start.1 = (bf16[1,8,1,8,128]{4,3,2,1,0:T(8,128)(2,1)S(1)}, bf16[1,8,1,8,128]{4,3,2,1,0:T(8,128)(2,1)S(1)}, u32[]{:S(2)}, u32[]{:S(2)}) collective-permute-start(bf16[1,8,1,8,128]{4,3,2,1,0:T(8,128)(2,1)S(1)} %get-tuple-element.116), channel_id=1, source_target_pairs={{1,0},{2,1},{3,2},{4,3},{5,4},{6,5},{7,6},{8,7},{9,8},{10,9},{11,1... | collective-permute-start | bytes 49160 | tf_op jit(solution)/shard_map/ppermute | solution.py:13
  73.5 3.5 %collective-permute-start.2 = (bf16[1,1,8,8,128]{4,3,2,1,0:T(8,128)(2,1)S(1)}, bf16[1,1,8,8,128]{4,3,2,1,0:T(8,128)(2,1)S(1)}, u32[]{:S(2)}, u32[]{:S(2)}) collective-permute-start(bf16[1,1,8,8,128]{4,3,2,1,0:T(8,128)(2,1)S(1)} %get-tuple-element.114), channel_id=1, source_target_pairs={{0,16},{16,32},{32,48},{1,17},{17,33},{33,49},{2,18},{18,34},{34,5... | collective-permute-start | bytes 49160 | tf_op jit(solution)/shard_map/ppermute | solution.py:12
  77.0 1.3 collective-permute-start.3
  78.7 4.0 %collective-permute-done.3 = bf16[1,1,8,8,128]{4,3,2,1,0:T(8,128)(2,1)S(1)} collective-permute-done((bf16[1,1,8,8,128]{4,3,2,1,0:T(8,128)(2,1)S(1)}, bf16[1,1,8,8,128]{4,3,2,1,0:T(8,128)(2,1)S(1)}, u32[]{:S(2)}, u32[]{:S(2)}) %collective-permute-start.3) | collective-permute-done | bytes 16416 | tf_op jit(solution)/shard_map/ppermute | solution.py:13
  83.5 1.1 fusion.66
  88.8 1.1 bitcast_dynamic-update-slice_fusion.6
  90.2 2.2 collective-permute-start.4
  92.4 4.9 %collective-permute-start.5 = (bf16[1,8,1,8,128]{4,3,2,1,0:T(8,128)(2,1)S(1)}, bf16[1,8,1,8,128]{4,3,2,1,0:T(8,128)(2,1)S(1)}, u32[]{:S(2)}, u32[]{:S(2)}) collective-permute-start(bf16[1,8,1,8,128]{4,3,2,1,0:T(8,128)(2,1)S(1)} %get-tuple-element.108), channel_id=1, source_target_pairs={{1,0},{2,1},{3,2},{4,3},{5,4},{6,5},{7,6},{8,7},{9,8},{10,9},{11,1... | collective-permute-start | bytes 49160 | tf_op jit(solution)/shard_map/ppermute | solution.py:13
  97.3 3.5 %collective-permute-start.6 = (bf16[1,1,8,8,128]{4,3,2,1,0:T(8,128)(2,1)S(1)}, bf16[1,1,8,8,128]{4,3,2,1,0:T(8,128)(2,1)S(1)}, u32[]{:S(2)}, u32[]{:S(2)}) collective-permute-start(bf16[1,1,8,8,128]{4,3,2,1,0:T(8,128)(2,1)S(1)} %get-tuple-element.106), channel_id=1, source_target_pairs={{0,16},{16,32},{32,48},{1,17},{17,33},{33,49},{2,18},{18,34},{34,5... | collective-permute-start | bytes 49160 | tf_op jit(solution)/shard_map/ppermute | solution.py:12
  100.8 1.3 collective-permute-start.7
  102.8 3.7 %collective-permute-done.7 = bf16[1,1,8,8,128]{4,3,2,1,0:T(8,128)(2,1)S(1)} collective-permute-done((bf16[1,1,8,8,128]{4,3,2,1,0:T(8,128)(2,1)S(1)}, bf16[1,1,8,8,128]{4,3,2,1,0:T(8,128)(2,1)S(1)}, u32[]{:S(2)}, u32[]{:S(2)}) %collective-permute-start.7) | collective-permute-done | bytes 16416 | tf_op jit(solution)/shard_map/ppermute | solution.py:13
  108.9 3.6 %collective-permute-start.10 = (bf16[1,1,8,8,128]{4,3,2,1,0:T(8,128)(2,1)S(1)}, bf16[1,1,8,8,128]{4,3,2,1,0:T(8,128)(2,1)S(1)}, u32[]{:S(2)}, u32[]{:S(2)}) collective-permute-start(bf16[1,1,8,8,128]{4,3,2,1,0:T(8,128)(2,1)S(1)} %get-tuple-element.98), channel_id=1, source_target_pairs={{0,16},{16,32},{32,48},{1,17},{17,33},{33,49},{2,18},{18,34},{34,5... | collective-permute-start | bytes 49160 | tf_op jit(solution)/shard_map/ppermute | solution.py:12
  112.5 1.3 collective-permute-start.11
  113.8 1.9 collective-permute-start.8
  115.7 5.1 %collective-permute-start.9 = (bf16[1,8,1,8,128]{4,3,2,1,0:T(8,128)(2,1)S(1)}, bf16[1,8,1,8,128]{4,3,2,1,0:T(8,128)(2,1)S(1)}, u32[]{:S(2)}, u32[]{:S(2)}) collective-permute-start(bf16[1,8,1,8,128]{4,3,2,1,0:T(8,128)(2,1)S(1)} %get-tuple-element.100), channel_id=1, source_target_pairs={{1,0},{2,1},{3,2},{4,3},{5,4},{6,5},{7,6},{8,7},{9,8},{10,9},{11,1... | collective-permute-start | bytes 49160 | tf_op jit(solution)/shard_map/ppermute | solution.py:13
  121.0 1.2 collective-permute-done.9
  125.2 1.9 collective-permute-start.12
  127.1 5.4 %collective-permute-start.13 = (bf16[1,8,1,8,128]{4,3,2,1,0:T(8,128)(2,1)S(1)}, bf16[1,8,1,8,128]{4,3,2,1,0:T(8,128)(2,1)S(1)}, u32[]{:S(2)}, u32[]{:S(2)}) collective-permute-start(bf16[1,8,1,8,128]{4,3,2,1,0:T(8,128)(2,1)S(1)} %get-tuple-element.92), channel_id=1, source_target_pairs={{1,0},{2,1},{3,2},{4,3},{5,4},{6,5},{7,6},{8,7},{9,8},{10,9},{11,1... | collective-permute-start | bytes 49160 | tf_op jit(solution)/shard_map/ppermute | solution.py:13
  132.5 4.6 %collective-permute-start.14 = (bf16[1,1,8,8,128]{4,3,2,1,0:T(8,128)(2,1)S(1)}, bf16[1,1,8,8,128]{4,3,2,1,0:T(8,128)(2,1)S(1)}, u32[]{:S(2)}, u32[]{:S(2)}) collective-permute-start(bf16[1,1,8,8,128]{4,3,2,1,0:T(8,128)(2,1)S(1)} %get-tuple-element.90), channel_id=1, source_target_pairs={{0,16},{16,32},{32,48},{1,17},{17,33},{33,49},{2,18},{18,34},{34,5... | collective-permute-start | bytes 49160 | tf_op jit(solution)/shard_map/ppermute | solution.py:12
  137.1 1.3 collective-permute-start.15
  139.0 3.7 %collective-permute-done.15 = bf16[1,1,8,8,128]{4,3,2,1,0:T(8,128)(2,1)S(1)} collective-permute-done((bf16[1,1,8,8,128]{4,3,2,1,0:T(8,128)(2,1)S(1)}, bf16[1,1,8,8,128]{4,3,2,1,0:T(8,128)(2,1)S(1)}, u32[]{:S(2)}, u32[]{:S(2)}) %collective-permute-start.15) | collective-permute-done | bytes 16416 | tf_op jit(solution)/shard_map/ppermute | solution.py:13
  145.1 1.9 collective-permute-start.16
  147.0 5.1 %collective-permute-start.17 = (bf16[1,8,1,8,128]{4,3,2,1,0:T(8,128)(2,1)S(1)}, bf16[1,8,1,8,128]{4,3,2,1,0:T(8,128)(2,1)S(1)}, u32[]{:S(2)}, u32[]{:S(2)}) collective-permute-start(bf16[1,8,1,8,128]{4,3,2,1,0:T(8,128)(2,1)S(1)} %get-tuple-element.84), channel_id=1, source_target_pairs={{1,0},{2,1},{3,2},{4,3},{5,4},{6,5},{7,6},{8,7},{9,8},{10,9},{11,1... | collective-permute-start | bytes 49160 | tf_op jit(solution)/shard_map/ppermute | solution.py:13
  152.2 1.9 collective-permute-start.18
  154.1 1.3 collective-permute-start.19
  156.1 3.7 %collective-permute-done.19 = bf16[1,1,8,8,128]{4,3,2,1,0:T(8,128)(2,1)S(1)} collective-permute-done((bf16[1,1,8,8,128]{4,3,2,1,0:T(8,128)(2,1)S(1)}, bf16[1,1,8,8,128]{4,3,2,1,0:T(8,128)(2,1)S(1)}, u32[]{:S(2)}, u32[]{:S(2)}) %collective-permute-start.19) | collective-permute-done | bytes 16416 | tf_op jit(solution)/shard_map/ppermute | solution.py:13
  162.2 1.9 collective-permute-start.20
  164.1 5.1 %collective-permute-start.21 = (bf16[1,8,1,8,128]{4,3,2,1,0:T(8,128)(2,1)S(1)}, bf16[1,8,1,8,128]{4,3,2,1,0:T(8,128)(2,1)S(1)}, u32[]{:S(2)}, u32[]{:S(2)}) collective-permute-start(bf16[1,8,1,8,128]{4,3,2,1,0:T(8,128)(2,1)S(1)} %get-tuple-element.76), channel_id=1, source_target_pairs={{1,0},{2,1},{3,2},{4,3},{5,4},{6,5},{7,6},{8,7},{9,8},{10,9},{11,1... | collective-permute-start | bytes 49160 | tf_op jit(solution)/shard_map/ppermute | solution.py:13
  169.2 1.9 collective-permute-start.22
  171.2 1.5 collective-permute-start.23
  173.3 3.5 %collective-permute-done.23 = bf16[1,1,8,8,128]{4,3,2,1,0:T(8,128)(2,1)S(1)} collective-permute-done((bf16[1,1,8,8,128]{4,3,2,1,0:T(8,128)(2,1)S(1)}, bf16[1,1,8,8,128]{4,3,2,1,0:T(8,128)(2,1)S(1)}, u32[]{:S(2)}, u32[]{:S(2)}) %collective-permute-start.23) | collective-permute-done | bytes 16416 | tf_op jit(solution)/shard_map/ppermute | solution.py:13
  179.2 1.9 collective-permute-start.24
  181.2 5.1 %collective-permute-start.25 = (bf16[1,8,1,8,128]{4,3,2,1,0:T(8,128)(2,1)S(1)}, bf16[1,8,1,8,128]{4,3,2,1,0:T(8,128)(2,1)S(1)}, u32[]{:S(2)}, u32[]{:S(2)}) collective-permute-start(bf16[1,8,1,8,128]{4,3,2,1,0:T(8,128)(2,1)S(1)} %get-tuple-element.68), channel_id=1, source_target_pairs={{1,0},{2,1},{3,2},{4,3},{5,4},{6,5},{7,6},{8,7},{9,8},{10,9},{11,1... | collective-permute-start | bytes 49160 | tf_op jit(solution)/shard_map/ppermute | solution.py:13
  186.3 1.9 collective-permute-start.26
  188.2 1.3 collective-permute-start.27
  190.2 3.7 %collective-permute-done.27 = bf16[1,1,8,8,128]{4,3,2,1,0:T(8,128)(2,1)S(1)} collective-permute-done((bf16[1,1,8,8,128]{4,3,2,1,0:T(8,128)(2,1)S(1)}, bf16[1,1,8,8,128]{4,3,2,1,0:T(8,128)(2,1)S(1)}, u32[]{:S(2)}, u32[]{:S(2)}) %collective-permute-start.27) | collective-permute-done | bytes 16416 | tf_op jit(solution)/shard_map/ppermute | solution.py:13
  196.3 1.9 collective-permute-start.28
  198.2 5.1 %collective-permute-start.29 = (bf16[1,8,1,8,128]{4,3,2,1,0:T(8,128)(2,1)S(1)}, bf16[1,8,1,8,128]{4,3,2,1,0:T(8,128)(2,1)S(1)}, u32[]{:S(2)}, u32[]{:S(2)}) collective-permute-start(bf16[1,8,1,8,128]{4,3,2,1,0:T(8,128)(2,1)S(1)} %get-tuple-element.60), channel_id=1, source_target_pairs={{1,0},{2,1},{3,2},{4,3},{5,4},{6,5},{7,6},{8,7},{9,8},{10,9},{11,1... | collective-permute-start | bytes 49160 | tf_op jit(solution)/shard_map/ppermute | solution.py:13
  203.3 1.9 collective-permute-start.30
  205.3 1.3 collective-permute-start.31
  207.2 3.7 %collective-permute-done.31 = bf16[1,1,8,8,128]{4,3,2,1,0:T(8,128)(2,1)S(1)} collective-permute-done((bf16[1,1,8,8,128]{4,3,2,1,0:T(8,128)(2,1)S(1)}, bf16[1,1,8,8,128]{4,3,2,1,0:T(8,128)(2,1)S(1)}, u32[]{:S(2)}, u32[]{:S(2)}) %collective-permute-start.31) | collective-permute-done | bytes 16416 | tf_op jit(solution)/shard_map/ppermute | solution.py:13
  213.0 19.1 %all_to_all.17 = bf16[8,1,8,8,8,128]{5,4,3,2,1,0:T(8,128)(2,1)S(1)} all-to-all(bf16[8,1,8,8,8,128]{5,4,3,2,1,0:T(8,128)(2,1)S(1)} %fusion.41), channel_id=1, replica_groups=mesh['section'=8,'frames'=4,'space'=16] {'section'}, dimensions={0} | all-to-all | bytes 2097152 | tf_op jit(solution)/shard_map/all_to_all | solution.py:80
  (208 shorter events, 30.7 us)
Async XLA Ops:
  6.5 31.5 %copy-start.4 = (bf16[1,128,128]{2,1,0:T(8,128)(2,1)S(1)}, bf16[1,128,128]{2,1,0:T(8,128)(2,1)}, u32[]{:S(2)}) copy-start(bf16[1,128,128]{2,1,0:T(8,128)(2,1)} %param.11) | copy-start | bytes 98308
  6.5 44.4 %copy-start.3 = (bf16[1,3,128,128]{3,2,1,0:T(8,128)(2,1)S(1)}, bf16[1,3,128,128]{3,2,1,0:T(8,128)(2,1)}, u32[]{:S(2)}) copy-start(bf16[1,3,128,128]{3,2,1,0:T(8,128)(2,1)} %param.10) | copy-start | bytes 294916
  6.5 76.9 %all-gather.2.cloned.1.call-start = ((), (), s32[]{:S(2)}) async-start(), calls=%async_computation.2 | async-start | bytes 2654208 | tf_op jit(solution)/shard_map/all_gather | solution.py:64
  7.3 57.0 %all-to-all-start = ((bf16[8,8,8,8,128]{4,3,2,1,0:T(8,128)(2,1)}), bf16[8,8,8,8,128]{4,3,2,1,0:T(8,128)(2,1)S(1)}, u32[]{:S(2)}, u32[]{:S(2)}) async-start(bf16[8,8,8,8,128]{4,3,2,1,0:T(8,128)(2,1)} %bitcast.664), calls=%async_computation | async-start | bytes 2097152 | tf_op jit(solution)/shard_map/all_to_all | solution.py:61
  66.4 12.0 %collective-permute-start = (bf16[1,8,1,8,128]{4,3,2,1,0:T(8,128)(2,1)S(1)}, bf16[1,8,1,8,128]{4,3,2,1,0:T(8,128)(2,1)S(1)}, u32[]{:S(2)}, u32[]{:S(2)}) collective-permute-start(bf16[1,8,1,8,128]{4,3,2,1,0:T(8,128)(2,1)S(1)} %get-tuple-element.115), channel_id=1, source_target_pairs={{0,1},{1,2},{2,3},{3,4},{4,5},{5,6},{6,7},{7,8},{8,9},{9,10},{10,1... | collective-permute-start | bytes 49160 | tf_op jit(solution)/shard_map/ppermute | solution.py:12
  69.8 8.7 %collective-permute-start.1 = (bf16[1,8,1,8,128]{4,3,2,1,0:T(8,128)(2,1)S(1)}, bf16[1,8,1,8,128]{4,3,2,1,0:T(8,128)(2,1)S(1)}, u32[]{:S(2)}, u32[]{:S(2)}) collective-permute-start(bf16[1,8,1,8,128]{4,3,2,1,0:T(8,128)(2,1)S(1)} %get-tuple-element.116), channel_id=1, source_target_pairs={{1,0},{2,1},{3,2},{4,3},{5,4},{6,5},{7,6},{8,7},{9,8},{10,9},{11,1... | collective-permute-start | bytes 49160 | tf_op jit(solution)/shard_map/ppermute | solution.py:13
  73.5 5.1 %collective-permute-start.2 = (bf16[1,1,8,8,128]{4,3,2,1,0:T(8,128)(2,1)S(1)}, bf16[1,1,8,8,128]{4,3,2,1,0:T(8,128)(2,1)S(1)}, u32[]{:S(2)}, u32[]{:S(2)}) collective-permute-start(bf16[1,1,8,8,128]{4,3,2,1,0:T(8,128)(2,1)S(1)} %get-tuple-element.114), channel_id=1, source_target_pairs={{0,16},{16,32},{32,48},{1,17},{17,33},{33,49},{2,18},{18,34},{34,5... | collective-permute-start | bytes 49160 | tf_op jit(solution)/shard_map/ppermute | solution.py:12
  77.0 5.6 %collective-permute-start.3 = (bf16[1,1,8,8,128]{4,3,2,1,0:T(8,128)(2,1)S(1)}, bf16[1,1,8,8,128]{4,3,2,1,0:T(8,128)(2,1)S(1)}, u32[]{:S(2)}, u32[]{:S(2)}) collective-permute-start(bf16[1,1,8,8,128]{4,3,2,1,0:T(8,128)(2,1)S(1)} %get-tuple-element.113), channel_id=1, source_target_pairs={{16,0},{32,16},{48,32},{17,1},{33,17},{49,33},{18,2},{34,18},{50,3... | collective-permute-start | bytes 49160 | tf_op jit(solution)/shard_map/ppermute | solution.py:13
  83.5 3.9 %copy-start = (bf16[8,9,128,128]{3,2,1,0:T(8,128)(2,1)S(1)}, bf16[8,9,128,128]{3,2,1,0:T(8,128)(2,1)}, u32[]{:S(2)}) copy-start(bf16[8,9,128,128]{3,2,1,0:T(8,128)(2,1)} %all-gather.2.cloned.1.call-done) | copy-start | bytes 7077892
  84.6 3.6 %copy-start.1 = (bf16[1,8,8,8,128]{4,3,2,1,0:T(8,128)(2,1)S(1)}, bf16[1,8,8,8,128]{4,3,2,1,0:T(8,128)(2,1)}, u32[]{:S(2)}) copy-start(bf16[1,8,8,8,128]{4,3,2,1,0:T(8,128)(2,1)} %get-tuple-element.111) | copy-start | bytes 393220
  87.4 1.1 copy-start.2
  90.2 12.1 %collective-permute-start.4 = (bf16[1,8,1,8,128]{4,3,2,1,0:T(8,128)(2,1)S(1)}, bf16[1,8,1,8,128]{4,3,2,1,0:T(8,128)(2,1)S(1)}, u32[]{:S(2)}, u32[]{:S(2)}) collective-permute-start(bf16[1,8,1,8,128]{4,3,2,1,0:T(8,128)(2,1)S(1)} %get-tuple-element.107), channel_id=1, source_target_pairs={{0,1},{1,2},{2,3},{3,4},{4,5},{5,6},{6,7},{7,8},{8,9},{9,10},{10,1... | collective-permute-start | bytes 49160 | tf_op jit(solution)/shard_map/ppermute | solution.py:12
  92.4 9.9 %collective-permute-start.5 = (bf16[1,8,1,8,128]{4,3,2,1,0:T(8,128)(2,1)S(1)}, bf16[1,8,1,8,128]{4,3,2,1,0:T(8,128)(2,1)S(1)}, u32[]{:S(2)}, u32[]{:S(2)}) collective-permute-start(bf16[1,8,1,8,128]{4,3,2,1,0:T(8,128)(2,1)S(1)} %get-tuple-element.108), channel_id=1, source_target_pairs={{1,0},{2,1},{3,2},{4,3},{5,4},{6,5},{7,6},{8,7},{9,8},{10,9},{11,1... | collective-permute-start | bytes 49160 | tf_op jit(solution)/shard_map/ppermute | solution.py:13
  97.3 5.5 %collective-permute-start.6 = (bf16[1,1,8,8,128]{4,3,2,1,0:T(8,128)(2,1)S(1)}, bf16[1,1,8,8,128]{4,3,2,1,0:T(8,128)(2,1)S(1)}, u32[]{:S(2)}, u32[]{:S(2)}) collective-permute-start(bf16[1,1,8,8,128]{4,3,2,1,0:T(8,128)(2,1)S(1)} %get-tuple-element.106), channel_id=1, source_target_pairs={{0,16},{16,32},{32,48},{1,17},{17,33},{33,49},{2,18},{18,34},{34,5... | collective-permute-start | bytes 49160 | tf_op jit(solution)/shard_map/ppermute | solution.py:12
  100.8 5.6 %collective-permute-start.7 = (bf16[1,1,8,8,128]{4,3,2,1,0:T(8,128)(2,1)S(1)}, bf16[1,1,8,8,128]{4,3,2,1,0:T(8,128)(2,1)S(1)}, u32[]{:S(2)}, u32[]{:S(2)}) collective-permute-start(bf16[1,1,8,8,128]{4,3,2,1,0:T(8,128)(2,1)S(1)} %get-tuple-element.105), channel_id=1, source_target_pairs={{16,0},{32,16},{48,32},{17,1},{33,17},{49,33},{18,2},{34,18},{50,3... | collective-permute-start | bytes 49160 | tf_op jit(solution)/shard_map/ppermute | solution.py:13
  108.9 13.8 %collective-permute-start.10 = (bf16[1,1,8,8,128]{4,3,2,1,0:T(8,128)(2,1)S(1)}, bf16[1,1,8,8,128]{4,3,2,1,0:T(8,128)(2,1)S(1)}, u32[]{:S(2)}, u32[]{:S(2)}) collective-permute-start(bf16[1,1,8,8,128]{4,3,2,1,0:T(8,128)(2,1)S(1)} %get-tuple-element.98), channel_id=1, source_target_pairs={{0,16},{16,32},{32,48},{1,17},{17,33},{33,49},{2,18},{18,34},{34,5... | collective-permute-start | bytes 49160 | tf_op jit(solution)/shard_map/ppermute | solution.py:12
  112.5 10.2 %collective-permute-start.11 = (bf16[1,1,8,8,128]{4,3,2,1,0:T(8,128)(2,1)S(1)}, bf16[1,1,8,8,128]{4,3,2,1,0:T(8,128)(2,1)S(1)}, u32[]{:S(2)}, u32[]{:S(2)}) collective-permute-start(bf16[1,1,8,8,128]{4,3,2,1,0:T(8,128)(2,1)S(1)} %get-tuple-element.97), channel_id=1, source_target_pairs={{16,0},{32,16},{48,32},{17,1},{33,17},{49,33},{18,2},{34,18},{50,3... | collective-permute-start | bytes 49160 | tf_op jit(solution)/shard_map/ppermute | solution.py:13
  113.8 7.2 %collective-permute-start.8 = (bf16[1,8,1,8,128]{4,3,2,1,0:T(8,128)(2,1)S(1)}, bf16[1,8,1,8,128]{4,3,2,1,0:T(8,128)(2,1)S(1)}, u32[]{:S(2)}, u32[]{:S(2)}) collective-permute-start(bf16[1,8,1,8,128]{4,3,2,1,0:T(8,128)(2,1)S(1)} %get-tuple-element.99), channel_id=1, source_target_pairs={{0,1},{1,2},{2,3},{3,4},{4,5},{5,6},{6,7},{7,8},{8,9},{9,10},{10,1... | collective-permute-start | bytes 49160 | tf_op jit(solution)/shard_map/ppermute | solution.py:12
  115.7 6.6 %collective-permute-start.9 = (bf16[1,8,1,8,128]{4,3,2,1,0:T(8,128)(2,1)S(1)}, bf16[1,8,1,8,128]{4,3,2,1,0:T(8,128)(2,1)S(1)}, u32[]{:S(2)}, u32[]{:S(2)}) collective-permute-start(bf16[1,8,1,8,128]{4,3,2,1,0:T(8,128)(2,1)S(1)} %get-tuple-element.100), channel_id=1, source_target_pairs={{1,0},{2,1},{3,2},{4,3},{5,4},{6,5},{7,6},{8,7},{9,8},{10,9},{11,1... | collective-permute-start | bytes 49160 | tf_op jit(solution)/shard_map/ppermute | solution.py:13
  125.2 13.4 %collective-permute-start.12 = (bf16[1,8,1,8,128]{4,3,2,1,0:T(8,128)(2,1)S(1)}, bf16[1,8,1,8,128]{4,3,2,1,0:T(8,128)(2,1)S(1)}, u32[]{:S(2)}, u32[]{:S(2)}) collective-permute-start(bf16[1,8,1,8,128]{4,3,2,1,0:T(8,128)(2,1)S(1)} %get-tuple-element.91), channel_id=1, source_target_pairs={{0,1},{1,2},{2,3},{3,4},{4,5},{5,6},{6,7},{7,8},{8,9},{9,10},{10,1... | collective-permute-start | bytes 49160 | tf_op jit(solution)/shard_map/ppermute | solution.py:12
  127.1 11.5 %collective-permute-start.13 = (bf16[1,8,1,8,128]{4,3,2,1,0:T(8,128)(2,1)S(1)}, bf16[1,8,1,8,128]{4,3,2,1,0:T(8,128)(2,1)S(1)}, u32[]{:S(2)}, u32[]{:S(2)}) collective-permute-start(bf16[1,8,1,8,128]{4,3,2,1,0:T(8,128)(2,1)S(1)} %get-tuple-element.92), channel_id=1, source_target_pairs={{1,0},{2,1},{3,2},{4,3},{5,4},{6,5},{7,6},{8,7},{9,8},{10,9},{11,1... | collective-permute-start | bytes 49160 | tf_op jit(solution)/shard_map/ppermute | solution.py:13
  132.5 6.5 %collective-permute-start.14 = (bf16[1,1,8,8,128]{4,3,2,1,0:T(8,128)(2,1)S(1)}, bf16[1,1,8,8,128]{4,3,2,1,0:T(8,128)(2,1)S(1)}, u32[]{:S(2)}, u32[]{:S(2)}) collective-permute-start(bf16[1,1,8,8,128]{4,3,2,1,0:T(8,128)(2,1)S(1)} %get-tuple-element.90), channel_id=1, source_target_pairs={{0,16},{16,32},{32,48},{1,17},{17,33},{33,49},{2,18},{18,34},{34,5... | collective-permute-start | bytes 49160 | tf_op jit(solution)/shard_map/ppermute | solution.py:12
  137.1 5.6 %collective-permute-start.15 = (bf16[1,1,8,8,128]{4,3,2,1,0:T(8,128)(2,1)S(1)}, bf16[1,1,8,8,128]{4,3,2,1,0:T(8,128)(2,1)S(1)}, u32[]{:S(2)}, u32[]{:S(2)}) collective-permute-start(bf16[1,1,8,8,128]{4,3,2,1,0:T(8,128)(2,1)S(1)} %get-tuple-element.89), channel_id=1, source_target_pairs={{16,0},{32,16},{48,32},{17,1},{33,17},{49,33},{18,2},{34,18},{50,3... | collective-permute-start | bytes 49160 | tf_op jit(solution)/shard_map/ppermute | solution.py:13
  145.1 10.5 %collective-permute-start.16 = (bf16[1,8,1,8,128]{4,3,2,1,0:T(8,128)(2,1)S(1)}, bf16[1,8,1,8,128]{4,3,2,1,0:T(8,128)(2,1)S(1)}, u32[]{:S(2)}, u32[]{:S(2)}) collective-permute-start(bf16[1,8,1,8,128]{4,3,2,1,0:T(8,128)(2,1)S(1)} %get-tuple-element.83), channel_id=1, source_target_pairs={{0,1},{1,2},{2,3},{3,4},{4,5},{5,6},{6,7},{7,8},{8,9},{9,10},{10,1... | collective-permute-start | bytes 49160 | tf_op jit(solution)/shard_map/ppermute | solution.py:12
  147.0 8.6 %collective-permute-start.17 = (bf16[1,8,1,8,128]{4,3,2,1,0:T(8,128)(2,1)S(1)}, bf16[1,8,1,8,128]{4,3,2,1,0:T(8,128)(2,1)S(1)}, u32[]{:S(2)}, u32[]{:S(2)}) collective-permute-start(bf16[1,8,1,8,128]{4,3,2,1,0:T(8,128)(2,1)S(1)} %get-tuple-element.84), channel_id=1, source_target_pairs={{1,0},{2,1},{3,2},{4,3},{5,4},{6,5},{7,6},{8,7},{9,8},{10,9},{11,1... | collective-permute-start | bytes 49160 | tf_op jit(solution)/shard_map/ppermute | solution.py:13
  152.2 3.9 %collective-permute-start.18 = (bf16[1,1,8,8,128]{4,3,2,1,0:T(8,128)(2,1)S(1)}, bf16[1,1,8,8,128]{4,3,2,1,0:T(8,128)(2,1)S(1)}, u32[]{:S(2)}, u32[]{:S(2)}) collective-permute-start(bf16[1,1,8,8,128]{4,3,2,1,0:T(8,128)(2,1)S(1)} %get-tuple-element.82), channel_id=1, source_target_pairs={{0,16},{16,32},{32,48},{1,17},{17,33},{33,49},{2,18},{18,34},{34,5... | collective-permute-start | bytes 49160 | tf_op jit(solution)/shard_map/ppermute | solution.py:12
  154.1 5.6 %collective-permute-start.19 = (bf16[1,1,8,8,128]{4,3,2,1,0:T(8,128)(2,1)S(1)}, bf16[1,1,8,8,128]{4,3,2,1,0:T(8,128)(2,1)S(1)}, u32[]{:S(2)}, u32[]{:S(2)}) collective-permute-start(bf16[1,1,8,8,128]{4,3,2,1,0:T(8,128)(2,1)S(1)} %get-tuple-element.81), channel_id=1, source_target_pairs={{16,0},{32,16},{48,32},{17,1},{33,17},{49,33},{18,2},{34,18},{50,3... | collective-permute-start | bytes 49160 | tf_op jit(solution)/shard_map/ppermute | solution.py:13
  162.2 10.6 %collective-permute-start.20 = (bf16[1,8,1,8,128]{4,3,2,1,0:T(8,128)(2,1)S(1)}, bf16[1,8,1,8,128]{4,3,2,1,0:T(8,128)(2,1)S(1)}, u32[]{:S(2)}, u32[]{:S(2)}) collective-permute-start(bf16[1,8,1,8,128]{4,3,2,1,0:T(8,128)(2,1)S(1)} %get-tuple-element.75), channel_id=1, source_target_pairs={{0,1},{1,2},{2,3},{3,4},{4,5},{5,6},{6,7},{7,8},{8,9},{9,10},{10,1... | collective-permute-start | bytes 49160 | tf_op jit(solution)/shard_map/ppermute | solution.py:12
  164.1 8.7 %collective-permute-start.21 = (bf16[1,8,1,8,128]{4,3,2,1,0:T(8,128)(2,1)S(1)}, bf16[1,8,1,8,128]{4,3,2,1,0:T(8,128)(2,1)S(1)}, u32[]{:S(2)}, u32[]{:S(2)}) collective-permute-start(bf16[1,8,1,8,128]{4,3,2,1,0:T(8,128)(2,1)S(1)} %get-tuple-element.76), channel_id=1, source_target_pairs={{1,0},{2,1},{3,2},{4,3},{5,4},{6,5},{7,6},{8,7},{9,8},{10,9},{11,1... | collective-permute-start | bytes 49160 | tf_op jit(solution)/shard_map/ppermute | solution.py:13
  169.2 4.0 %collective-permute-start.22 = (bf16[1,1,8,8,128]{4,3,2,1,0:T(8,128)(2,1)S(1)}, bf16[1,1,8,8,128]{4,3,2,1,0:T(8,128)(2,1)S(1)}, u32[]{:S(2)}, u32[]{:S(2)}) collective-permute-start(bf16[1,1,8,8,128]{4,3,2,1,0:T(8,128)(2,1)S(1)} %get-tuple-element.74), channel_id=1, source_target_pairs={{0,16},{16,32},{32,48},{1,17},{17,33},{33,49},{2,18},{18,34},{34,5... | collective-permute-start | bytes 49160 | tf_op jit(solution)/shard_map/ppermute | solution.py:12
  171.2 5.6 %collective-permute-start.23 = (bf16[1,1,8,8,128]{4,3,2,1,0:T(8,128)(2,1)S(1)}, bf16[1,1,8,8,128]{4,3,2,1,0:T(8,128)(2,1)S(1)}, u32[]{:S(2)}, u32[]{:S(2)}) collective-permute-start(bf16[1,1,8,8,128]{4,3,2,1,0:T(8,128)(2,1)S(1)} %get-tuple-element.73), channel_id=1, source_target_pairs={{16,0},{32,16},{48,32},{17,1},{33,17},{49,33},{18,2},{34,18},{50,3... | collective-permute-start | bytes 49160 | tf_op jit(solution)/shard_map/ppermute | solution.py:13
  179.2 10.5 %collective-permute-start.24 = (bf16[1,8,1,8,128]{4,3,2,1,0:T(8,128)(2,1)S(1)}, bf16[1,8,1,8,128]{4,3,2,1,0:T(8,128)(2,1)S(1)}, u32[]{:S(2)}, u32[]{:S(2)}) collective-permute-start(bf16[1,8,1,8,128]{4,3,2,1,0:T(8,128)(2,1)S(1)} %get-tuple-element.67), channel_id=1, source_target_pairs={{0,1},{1,2},{2,3},{3,4},{4,5},{5,6},{6,7},{7,8},{8,9},{9,10},{10,1... | collective-permute-start | bytes 49160 | tf_op jit(solution)/shard_map/ppermute | solution.py:12
  181.2 8.6 %collective-permute-start.25 = (bf16[1,8,1,8,128]{4,3,2,1,0:T(8,128)(2,1)S(1)}, bf16[1,8,1,8,128]{4,3,2,1,0:T(8,128)(2,1)S(1)}, u32[]{:S(2)}, u32[]{:S(2)}) collective-permute-start(bf16[1,8,1,8,128]{4,3,2,1,0:T(8,128)(2,1)S(1)} %get-tuple-element.68), channel_id=1, source_target_pairs={{1,0},{2,1},{3,2},{4,3},{5,4},{6,5},{7,6},{8,7},{9,8},{10,9},{11,1... | collective-permute-start | bytes 49160 | tf_op jit(solution)/shard_map/ppermute | solution.py:13
  186.3 3.9 %collective-permute-start.26 = (bf16[1,1,8,8,128]{4,3,2,1,0:T(8,128)(2,1)S(1)}, bf16[1,1,8,8,128]{4,3,2,1,0:T(8,128)(2,1)S(1)}, u32[]{:S(2)}, u32[]{:S(2)}) collective-permute-start(bf16[1,1,8,8,128]{4,3,2,1,0:T(8,128)(2,1)S(1)} %get-tuple-element.66), channel_id=1, source_target_pairs={{0,16},{16,32},{32,48},{1,17},{17,33},{33,49},{2,18},{18,34},{34,5... | collective-permute-start | bytes 49160 | tf_op jit(solution)/shard_map/ppermute | solution.py:12
  188.2 5.6 %collective-permute-start.27 = (bf16[1,1,8,8,128]{4,3,2,1,0:T(8,128)(2,1)S(1)}, bf16[1,1,8,8,128]{4,3,2,1,0:T(8,128)(2,1)S(1)}, u32[]{:S(2)}, u32[]{:S(2)}) collective-permute-start(bf16[1,1,8,8,128]{4,3,2,1,0:T(8,128)(2,1)S(1)} %get-tuple-element.65), channel_id=1, source_target_pairs={{16,0},{32,16},{48,32},{17,1},{33,17},{49,33},{18,2},{34,18},{50,3... | collective-permute-start | bytes 49160 | tf_op jit(solution)/shard_map/ppermute | solution.py:13
  196.3 10.5 %collective-permute-start.28 = (bf16[1,8,1,8,128]{4,3,2,1,0:T(8,128)(2,1)S(1)}, bf16[1,8,1,8,128]{4,3,2,1,0:T(8,128)(2,1)S(1)}, u32[]{:S(2)}, u32[]{:S(2)}) collective-permute-start(bf16[1,8,1,8,128]{4,3,2,1,0:T(8,128)(2,1)S(1)} %get-tuple-element.59), channel_id=1, source_target_pairs={{0,1},{1,2},{2,3},{3,4},{4,5},{5,6},{6,7},{7,8},{8,9},{9,10},{10,1... | collective-permute-start | bytes 49160 | tf_op jit(solution)/shard_map/ppermute | solution.py:12
  198.2 8.6 %collective-permute-start.29 = (bf16[1,8,1,8,128]{4,3,2,1,0:T(8,128)(2,1)S(1)}, bf16[1,8,1,8,128]{4,3,2,1,0:T(8,128)(2,1)S(1)}, u32[]{:S(2)}, u32[]{:S(2)}) collective-permute-start(bf16[1,8,1,8,128]{4,3,2,1,0:T(8,128)(2,1)S(1)} %get-tuple-element.60), channel_id=1, source_target_pairs={{1,0},{2,1},{3,2},{4,3},{5,4},{6,5},{7,6},{8,7},{9,8},{10,9},{11,1... | collective-permute-start | bytes 49160 | tf_op jit(solution)/shard_map/ppermute | solution.py:13
  203.3 3.9 %collective-permute-start.30 = (bf16[1,1,8,8,128]{4,3,2,1,0:T(8,128)(2,1)S(1)}, bf16[1,1,8,8,128]{4,3,2,1,0:T(8,128)(2,1)S(1)}, u32[]{:S(2)}, u32[]{:S(2)}) collective-permute-start(bf16[1,1,8,8,128]{4,3,2,1,0:T(8,128)(2,1)S(1)} %get-tuple-element.58), channel_id=1, source_target_pairs={{0,16},{16,32},{32,48},{1,17},{17,33},{33,49},{2,18},{18,34},{34,5... | collective-permute-start | bytes 49160 | tf_op jit(solution)/shard_map/ppermute | solution.py:12
  205.3 5.6 %collective-permute-start.31 = (bf16[1,1,8,8,128]{4,3,2,1,0:T(8,128)(2,1)S(1)}, bf16[1,1,8,8,128]{4,3,2,1,0:T(8,128)(2,1)S(1)}, u32[]{:S(2)}, u32[]{:S(2)}) collective-permute-start(bf16[1,1,8,8,128]{4,3,2,1,0:T(8,128)(2,1)S(1)} %get-tuple-element.57), channel_id=1, source_target_pairs={{16,0},{32,16},{48,32},{17,1},{33,17},{49,33},{18,2},{34,18},{50,3... | collective-permute-start | bytes 49160 | tf_op jit(solution)/shard_map/ppermute | solution.py:13
Sparse Core Ops, SparseCore 0:
  9.5 33.4 all-gather.1

commit v2 on v1

--- a/solution.py
+++ b/solution.py
@@ -60,20 +60,24 @@
     per_device = video_count // sections
     noise_t = lax.all_to_all(section_noise[0], "section", 0, 0, tiled=True)
     noise_t = noise_t.reshape((sections, per_device) + noise_t.shape[1:])
-    levels = lax.all_gather(noise_levels, "section", tiled=True)
-    spatial = lax.all_gather(spatial_kernel, "section", tiled=True)
-    temporal = lax.all_gather(temporal_kernel, "section", tiled=True)
-    out_weight = lax.all_gather(output_weight, "section", tiled=True)
+    channels = spatial_kernel.shape[-1]
+    level_slab = jnp.broadcast_to(
+        noise_levels.reshape(1, 1, 1, 1), (1, 1, channels, channels)
+    ).astype(spatial_kernel.dtype)
+    packed = jnp.concatenate(
+        [spatial_kernel, temporal_kernel, output_weight[:, None], level_slab], axis=1
+    )
+    packed = lax.all_gather(packed, "section", tiled=True)
     incoming = lax.dynamic_slice_in_dim(base_frames, place * per_device, per_device, 0)
     results = []
     for k in range(sections):
         incoming = denoise(
             incoming,
             noise_t[k],
-            levels[k].astype(jnp.float32),
-            spatial[k],
-            temporal[k],
-            out_weight[k],
+            packed[k, 13, 0, 0].astype(jnp.float32),
+            packed[k, 0:9],
+            packed[k, 9:12],
+            packed[k, 12],
         )
         results.append(incoming)
     stacked = jnp.stack(results)

time: 241 us -> 230 us (0.954)
  the two profiles are of different devices: /device:TPU:384 before, /device:TPU:128 now
where the time goes in v2:
time: 230 us; the launch traced here: 228 us
  starting transfers between devices  96.3 us (42%)
  waiting for transfers between devices  59.9 us (26%)
  matrix products  21.6 us (9%)
  between operations  20.9 us (9%)
  blocking collectives  18.8 us (8%)
  other arithmetic  7.54 us (3%)
  local copies, waits for them, and re-layouts  3.31 us (1%)
    ppermute x16, starting transfers between devices, shift_in(): high = lax.ppermute(lax.slice_in_dim(block, 0, 1, axis=dim), axis, backward)  46.8 us
    ppermute x16, starting transfers between devices, shift_in(): lax.ppermute(lax.slice_in_dim(block, size - 1, size, axis=dim), axis, for...  45.1 us
    all_gather x1, waiting for transfers between devices, on_device(): packed = lax.all_gather(packed, 'section', tiled=True)  36.6 us
    ppermute x16, waiting for transfers between devices, shift_in(): high = lax.ppermute(lax.slice_in_dim(block, 0, 1, axis=dim), axis, backward)  23.2 us
    all_to_all x1, blocking collectives, on_device(): return lax.all_to_all(stacked, 'section', 0, 1, tiled=True)  18.8 us
    dot_general x72, matrix products, denoise(): jnp.dot(shifted_view.reshape(-1, channels), spatial[tap_index], preferred...  13.8 us
    dot_general x24, matrix products, denoise(): jnp.dot(shifted_view.reshape(-1, channels), temporal[tap_index], preferre...  5.21 us
  transfers between devices with their start and end apart: 34, of which 8 were waited for; matrix products, arithmetic and copies ran while one was open for 3% of the time, Pallas kernels for 0%

profile of v2, /device:TPU:128, one launch (start us, length us, event | category | flops | bytes accessed | tf_op | source)
XLA Modules:
  0.0 228.3 jit_solution(11816875572995739471)
XLA Ops:
  7.3 1.9 maximum_maximum_fusion
  9.2 4.3 %all-to-all-start = ((bf16[8,8,8,8,128]{4,3,2,1,0:T(8,128)(2,1)}), bf16[8,8,8,8,128]{4,3,2,1,0:T(8,128)(2,1)S(1)}, u32[]{:S(2)}, u32[]{:S(2)}) async-start(bf16[8,8,8,8,128]{4,3,2,1,0:T(8,128)(2,1)} %bitcast.665), calls=%async_computation | async-start | bytes 2097152 | tf_op jit(solution)/shard_map/all_to_all | solution.py:61
  13.5 36.6 %all-gather.2.cloned.1.call-done = bf16[8,14,128,128]{3,2,1,0:T(8,128)(2,1)} async-done(((bf16[1,14,128,128]{3,2,1,0:T(8,128)(2,1)}), bf16[8,14,128,128]{3,2,1,0:T(8,128)(2,1)}) %all-gather.2.cloned.1.call-update) | async-done | bytes 3670032 | tf_op jit(solution)/shard_map/all_gather | solution.py:70
  50.1 1.3 fusion.67
  52.1 1.1 multiply_reduce_fusion.7
  53.2 1.0 multiply_convert_fusion.15
  54.2 3.5 %collective-permute-start = (bf16[1,8,1,8,128]{4,3,2,1,0:T(8,128)(2,1)S(1)}, bf16[1,8,1,8,128]{4,3,2,1,0:T(8,128)(2,1)S(1)}, u32[]{:S(2)}, u32[]{:S(2)}) collective-permute-start(bf16[1,8,1,8,128]{4,3,2,1,0:T(8,128)(2,1)S(1)} %get-tuple-element.123), channel_id=1, source_target_pairs={{0,1},{1,2},{2,3},{3,4},{4,5},{5,6},{6,7},{7,8},{8,9},{9,10},{10,1... | collective-permute-start | bytes 49160 | tf_op jit(solution)/shard_map/ppermute | solution.py:12
  57.7 3.6 %collective-permute-start.1 = (bf16[1,8,1,8,128]{4,3,2,1,0:T(8,128)(2,1)S(1)}, bf16[1,8,1,8,128]{4,3,2,1,0:T(8,128)(2,1)S(1)}, u32[]{:S(2)}, u32[]{:S(2)}) collective-permute-start(bf16[1,8,1,8,128]{4,3,2,1,0:T(8,128)(2,1)S(1)} %get-tuple-element.124), channel_id=1, source_target_pairs={{1,0},{2,1},{3,2},{4,3},{5,4},{6,5},{7,6},{8,7},{9,8},{10,9},{11,1... | collective-permute-start | bytes 49160 | tf_op jit(solution)/shard_map/ppermute | solution.py:13
  61.3 3.4 %collective-permute-start.2 = (bf16[1,1,8,8,128]{4,3,2,1,0:T(8,128)(2,1)S(1)}, bf16[1,1,8,8,128]{4,3,2,1,0:T(8,128)(2,1)S(1)}, u32[]{:S(2)}, u32[]{:S(2)}) collective-permute-start(bf16[1,1,8,8,128]{4,3,2,1,0:T(8,128)(2,1)S(1)} %get-tuple-element.122), channel_id=1, source_target_pairs={{0,16},{16,32},{32,48},{1,17},{17,33},{33,49},{2,18},{18,34},{34,5... | collective-permute-start | bytes 49160 | tf_op jit(solution)/shard_map/ppermute | solution.py:12
  64.7 1.3 collective-permute-start.3
  71.7 1.1 fusion.66
  75.5 1.1 bitcast_dynamic-update-slice_fusion.6
  76.9 2.2 collective-permute-start.4
  79.2 4.8 %collective-permute-start.5 = (bf16[1,8,1,8,128]{4,3,2,1,0:T(8,128)(2,1)S(1)}, bf16[1,8,1,8,128]{4,3,2,1,0:T(8,128)(2,1)S(1)}, u32[]{:S(2)}, u32[]{:S(2)}) collective-permute-start(bf16[1,8,1,8,128]{4,3,2,1,0:T(8,128)(2,1)S(1)} %get-tuple-element.116), channel_id=1, source_target_pairs={{1,0},{2,1},{3,2},{4,3},{5,4},{6,5},{7,6},{8,7},{9,8},{10,9},{11,1... | collective-permute-start | bytes 49160 | tf_op jit(solution)/shard_map/ppermute | solution.py:13
  84.0 4.5 %collective-permute-start.6 = (bf16[1,1,8,8,128]{4,3,2,1,0:T(8,128)(2,1)S(1)}, bf16[1,1,8,8,128]{4,3,2,1,0:T(8,128)(2,1)S(1)}, u32[]{:S(2)}, u32[]{:S(2)}) collective-permute-start(bf16[1,1,8,8,128]{4,3,2,1,0:T(8,128)(2,1)S(1)} %get-tuple-element.114), channel_id=1, source_target_pairs={{0,16},{16,32},{32,48},{1,17},{17,33},{33,49},{2,18},{18,34},{34,5... | collective-permute-start | bytes 49160 | tf_op jit(solution)/shard_map/ppermute | solution.py:12
  88.5 1.3 collective-permute-start.7
  90.5 3.7 %collective-permute-done.7 = bf16[1,1,8,8,128]{4,3,2,1,0:T(8,128)(2,1)S(1)} collective-permute-done((bf16[1,1,8,8,128]{4,3,2,1,0:T(8,128)(2,1)S(1)}, bf16[1,1,8,8,128]{4,3,2,1,0:T(8,128)(2,1)S(1)}, u32[]{:S(2)}, u32[]{:S(2)}) %collective-permute-start.7) | collective-permute-done | bytes 16416 | tf_op jit(solution)/shard_map/ppermute | solution.py:13
  96.6 3.4 %collective-permute-start.10 = (bf16[1,1,8,8,128]{4,3,2,1,0:T(8,128)(2,1)S(1)}, bf16[1,1,8,8,128]{4,3,2,1,0:T(8,128)(2,1)S(1)}, u32[]{:S(2)}, u32[]{:S(2)}) collective-permute-start(bf16[1,1,8,8,128]{4,3,2,1,0:T(8,128)(2,1)S(1)} %get-tuple-element.106), channel_id=1, source_target_pairs={{0,16},{16,32},{32,48},{1,17},{17,33},{33,49},{2,18},{18,34},{34,5... | collective-permute-start | bytes 49160 | tf_op jit(solution)/shard_map/ppermute | solution.py:12
  100.0 1.3 collective-permute-start.11
  101.3 1.9 collective-permute-start.8
  103.2 5.1 %collective-permute-start.9 = (bf16[1,8,1,8,128]{4,3,2,1,0:T(8,128)(2,1)S(1)}, bf16[1,8,1,8,128]{4,3,2,1,0:T(8,128)(2,1)S(1)}, u32[]{:S(2)}, u32[]{:S(2)}) collective-permute-start(bf16[1,8,1,8,128]{4,3,2,1,0:T(8,128)(2,1)S(1)} %get-tuple-element.108), channel_id=1, source_target_pairs={{1,0},{2,1},{3,2},{4,3},{5,4},{6,5},{7,6},{8,7},{9,8},{10,9},{11,1... | collective-permute-start | bytes 49160 | tf_op jit(solution)/shard_map/ppermute | solution.py:13
  108.6 1.2 collective-permute-done.9
  112.7 3.2 %collective-permute-start.12 = (bf16[1,8,1,8,128]{4,3,2,1,0:T(8,128)(2,1)S(1)}, bf16[1,8,1,8,128]{4,3,2,1,0:T(8,128)(2,1)S(1)}, u32[]{:S(2)}, u32[]{:S(2)}) collective-permute-start(bf16[1,8,1,8,128]{4,3,2,1,0:T(8,128)(2,1)S(1)} %get-tuple-element.99), channel_id=1, source_target_pairs={{0,1},{1,2},{2,3},{3,4},{4,5},{5,6},{6,7},{7,8},{8,9},{9,10},{10,1... | collective-permute-start | bytes 49160 | tf_op jit(solution)/shard_map/ppermute | solution.py:12
  115.8 4.2 %collective-permute-start.13 = (bf16[1,8,1,8,128]{4,3,2,1,0:T(8,128)(2,1)S(1)}, bf16[1,8,1,8,128]{4,3,2,1,0:T(8,128)(2,1)S(1)}, u32[]{:S(2)}, u32[]{:S(2)}) collective-permute-start(bf16[1,8,1,8,128]{4,3,2,1,0:T(8,128)(2,1)S(1)} %get-tuple-element.100), channel_id=1, source_target_pairs={{1,0},{2,1},{3,2},{4,3},{5,4},{6,5},{7,6},{8,7},{9,8},{10,9},{11,1... | collective-permute-start | bytes 49160 | tf_op jit(solution)/shard_map/ppermute | solution.py:13
  120.0 4.5 %collective-permute-start.14 = (bf16[1,1,8,8,128]{4,3,2,1,0:T(8,128)(2,1)S(1)}, bf16[1,1,8,8,128]{4,3,2,1,0:T(8,128)(2,1)S(1)}, u32[]{:S(2)}, u32[]{:S(2)}) collective-permute-start(bf16[1,1,8,8,128]{4,3,2,1,0:T(8,128)(2,1)S(1)} %get-tuple-element.98), channel_id=1, source_target_pairs={{0,16},{16,32},{32,48},{1,17},{17,33},{33,49},{2,18},{18,34},{34,5... | collective-permute-start | bytes 49160 | tf_op jit(solution)/shard_map/ppermute | solution.py:12
  124.6 1.3 collective-permute-start.15
  126.5 3.7 %collective-permute-done.15 = bf16[1,1,8,8,128]{4,3,2,1,0:T(8,128)(2,1)S(1)} collective-permute-done((bf16[1,1,8,8,128]{4,3,2,1,0:T(8,128)(2,1)S(1)}, bf16[1,1,8,8,128]{4,3,2,1,0:T(8,128)(2,1)S(1)}, u32[]{:S(2)}, u32[]{:S(2)}) %collective-permute-start.15) | collective-permute-done | bytes 16416 | tf_op jit(solution)/shard_map/ppermute | solution.py:13
  132.6 2.9 %collective-permute-start.16 = (bf16[1,8,1,8,128]{4,3,2,1,0:T(8,128)(2,1)S(1)}, bf16[1,8,1,8,128]{4,3,2,1,0:T(8,128)(2,1)S(1)}, u32[]{:S(2)}, u32[]{:S(2)}) collective-permute-start(bf16[1,8,1,8,128]{4,3,2,1,0:T(8,128)(2,1)S(1)} %get-tuple-element.91), channel_id=1, source_target_pairs={{0,1},{1,2},{2,3},{3,4},{4,5},{5,6},{6,7},{7,8},{8,9},{9,10},{10,1... | collective-permute-start | bytes 49160 | tf_op jit(solution)/shard_map/ppermute | solution.py:12
  135.5 4.2 %collective-permute-start.17 = (bf16[1,8,1,8,128]{4,3,2,1,0:T(8,128)(2,1)S(1)}, bf16[1,8,1,8,128]{4,3,2,1,0:T(8,128)(2,1)S(1)}, u32[]{:S(2)}, u32[]{:S(2)}) collective-permute-start(bf16[1,8,1,8,128]{4,3,2,1,0:T(8,128)(2,1)S(1)} %get-tuple-element.92), channel_id=1, source_target_pairs={{1,0},{2,1},{3,2},{4,3},{5,4},{6,5},{7,6},{8,7},{9,8},{10,9},{11,1... | collective-permute-start | bytes 49160 | tf_op jit(solution)/shard_map/ppermute | solution.py:13
  139.7 3.1 %collective-permute-start.18 = (bf16[1,1,8,8,128]{4,3,2,1,0:T(8,128)(2,1)S(1)}, bf16[1,1,8,8,128]{4,3,2,1,0:T(8,128)(2,1)S(1)}, u32[]{:S(2)}, u32[]{:S(2)}) collective-permute-start(bf16[1,1,8,8,128]{4,3,2,1,0:T(8,128)(2,1)S(1)} %get-tuple-element.90), channel_id=1, source_target_pairs={{0,16},{16,32},{32,48},{1,17},{17,33},{33,49},{2,18},{18,34},{34,5... | collective-permute-start | bytes 49160 | tf_op jit(solution)/shard_map/ppermute | solution.py:12
  142.8 1.3 collective-permute-start.19
  144.7 3.7 %collective-permute-done.19 = bf16[1,1,8,8,128]{4,3,2,1,0:T(8,128)(2,1)S(1)} collective-permute-done((bf16[1,1,8,8,128]{4,3,2,1,0:T(8,128)(2,1)S(1)}, bf16[1,1,8,8,128]{4,3,2,1,0:T(8,128)(2,1)S(1)}, u32[]{:S(2)}, u32[]{:S(2)}) %collective-permute-start.19) | collective-permute-done | bytes 16416 | tf_op jit(solution)/shard_map/ppermute | solution.py:13
  150.8 2.9 %collective-permute-start.20 = (bf16[1,8,1,8,128]{4,3,2,1,0:T(8,128)(2,1)S(1)}, bf16[1,8,1,8,128]{4,3,2,1,0:T(8,128)(2,1)S(1)}, u32[]{:S(2)}, u32[]{:S(2)}) collective-permute-start(bf16[1,8,1,8,128]{4,3,2,1,0:T(8,128)(2,1)S(1)} %get-tuple-element.83), channel_id=1, source_target_pairs={{0,1},{1,2},{2,3},{3,4},{4,5},{5,6},{6,7},{7,8},{8,9},{9,10},{10,1... | collective-permute-start | bytes 49160 | tf_op jit(solution)/shard_map/ppermute | solution.py:12
  153.8 4.2 %collective-permute-start.21 = (bf16[1,8,1,8,128]{4,3,2,1,0:T(8,128)(2,1)S(1)}, bf16[1,8,1,8,128]{4,3,2,1,0:T(8,128)(2,1)S(1)}, u32[]{:S(2)}, u32[]{:S(2)}) collective-permute-start(bf16[1,8,1,8,128]{4,3,2,1,0:T(8,128)(2,1)S(1)} %get-tuple-element.84), channel_id=1, source_target_pairs={{1,0},{2,1},{3,2},{4,3},{5,4},{6,5},{7,6},{8,7},{9,8},{10,9},{11,1... | collective-permute-start | bytes 49160 | tf_op jit(solution)/shard_map/ppermute | solution.py:13
  157.9 1.9 collective-permute-start.22
  159.8 1.3 collective-permute-start.23
  161.8 3.7 %collective-permute-done.23 = bf16[1,1,8,8,128]{4,3,2,1,0:T(8,128)(2,1)S(1)} collective-permute-done((bf16[1,1,8,8,128]{4,3,2,1,0:T(8,128)(2,1)S(1)}, bf16[1,1,8,8,128]{4,3,2,1,0:T(8,128)(2,1)S(1)}, u32[]{:S(2)}, u32[]{:S(2)}) %collective-permute-start.23) | collective-permute-done | bytes 16416 | tf_op jit(solution)/shard_map/ppermute | solution.py:13
  167.9 1.9 collective-permute-start.24
  169.8 5.1 %collective-permute-start.25 = (bf16[1,8,1,8,128]{4,3,2,1,0:T(8,128)(2,1)S(1)}, bf16[1,8,1,8,128]{4,3,2,1,0:T(8,128)(2,1)S(1)}, u32[]{:S(2)}, u32[]{:S(2)}) collective-permute-start(bf16[1,8,1,8,128]{4,3,2,1,0:T(8,128)(2,1)S(1)} %get-tuple-element.76), channel_id=1, source_target_pairs={{1,0},{2,1},{3,2},{4,3},{5,4},{6,5},{7,6},{8,7},{9,8},{10,9},{11,1... | collective-permute-start | bytes 49160 | tf_op jit(solution)/shard_map/ppermute | solution.py:13
  175.0 1.9 collective-permute-start.26
  176.9 1.5 collective-permute-start.27
  179.0 3.5 %collective-permute-done.27 = bf16[1,1,8,8,128]{4,3,2,1,0:T(8,128)(2,1)S(1)} collective-permute-done((bf16[1,1,8,8,128]{4,3,2,1,0:T(8,128)(2,1)S(1)}, bf16[1,1,8,8,128]{4,3,2,1,0:T(8,128)(2,1)S(1)}, u32[]{:S(2)}, u32[]{:S(2)}) %collective-permute-start.27) | collective-permute-done | bytes 16416 | tf_op jit(solution)/shard_map/ppermute | solution.py:13
  185.0 1.9 collective-permute-start.28
  186.9 5.1 %collective-permute-start.29 = (bf16[1,8,1,8,128]{4,3,2,1,0:T(8,128)(2,1)S(1)}, bf16[1,8,1,8,128]{4,3,2,1,0:T(8,128)(2,1)S(1)}, u32[]{:S(2)}, u32[]{:S(2)}) collective-permute-start(bf16[1,8,1,8,128]{4,3,2,1,0:T(8,128)(2,1)S(1)} %get-tuple-element.68), channel_id=1, source_target_pairs={{1,0},{2,1},{3,2},{4,3},{5,4},{6,5},{7,6},{8,7},{9,8},{10,9},{11,1... | collective-permute-start | bytes 49160 | tf_op jit(solution)/shard_map/ppermute | solution.py:13
  192.0 1.9 collective-permute-start.30
  194.0 1.3 collective-permute-start.31
  195.9 3.7 %collective-permute-done.31 = bf16[1,1,8,8,128]{4,3,2,1,0:T(8,128)(2,1)S(1)} collective-permute-done((bf16[1,1,8,8,128]{4,3,2,1,0:T(8,128)(2,1)S(1)}, bf16[1,1,8,8,128]{4,3,2,1,0:T(8,128)(2,1)S(1)}, u32[]{:S(2)}, u32[]{:S(2)}) %collective-permute-start.31) | collective-permute-done | bytes 16416 | tf_op jit(solution)/shard_map/ppermute | solution.py:13
  201.7 18.8 %all_to_all.17 = bf16[8,1,8,8,8,128]{5,4,3,2,1,0:T(8,128)(2,1)S(1)} all-to-all(bf16[8,1,8,8,8,128]{5,4,3,2,1,0:T(8,128)(2,1)S(1)} %fusion.41), channel_id=1, replica_groups=mesh['section'=8,'frames'=4,'space'=16] {'section'}, dimensions={0} | all-to-all | bytes 2097152 | tf_op jit(solution)/shard_map/all_to_all | solution.py:84
  (196 shorter events, 25.0 us)
Async XLA Ops:
  6.5 43.6 %all-gather.2.cloned.1.call-start = ((), (), s32[]{:S(2)}) async-start(), calls=%async_computation.2 | async-start | bytes 4128768 | tf_op jit(solution)/shard_map/all_gather | solution.py:70
  9.2 42.9 %all-to-all-start = ((bf16[8,8,8,8,128]{4,3,2,1,0:T(8,128)(2,1)}), bf16[8,8,8,8,128]{4,3,2,1,0:T(8,128)(2,1)S(1)}, u32[]{:S(2)}, u32[]{:S(2)}) async-start(bf16[8,8,8,8,128]{4,3,2,1,0:T(8,128)(2,1)} %bitcast.665), calls=%async_computation | async-start | bytes 2097152 | tf_op jit(solution)/shard_map/all_to_all | solution.py:61
  54.2 17.2 %collective-permute-start = (bf16[1,8,1,8,128]{4,3,2,1,0:T(8,128)(2,1)S(1)}, bf16[1,8,1,8,128]{4,3,2,1,0:T(8,128)(2,1)S(1)}, u32[]{:S(2)}, u32[]{:S(2)}) collective-permute-start(bf16[1,8,1,8,128]{4,3,2,1,0:T(8,128)(2,1)S(1)} %get-tuple-element.123), channel_id=1, source_target_pairs={{0,1},{1,2},{2,3},{3,4},{4,5},{5,6},{6,7},{7,8},{8,9},{9,10},{10,1... | collective-permute-start | bytes 49160 | tf_op jit(solution)/shard_map/ppermute | solution.py:12
  57.7 13.7 %collective-permute-start.1 = (bf16[1,8,1,8,128]{4,3,2,1,0:T(8,128)(2,1)S(1)}, bf16[1,8,1,8,128]{4,3,2,1,0:T(8,128)(2,1)S(1)}, u32[]{:S(2)}, u32[]{:S(2)}) collective-permute-start(bf16[1,8,1,8,128]{4,3,2,1,0:T(8,128)(2,1)S(1)} %get-tuple-element.124), channel_id=1, source_target_pairs={{1,0},{2,1},{3,2},{4,3},{5,4},{6,5},{7,6},{8,7},{9,8},{10,9},{11,1... | collective-permute-start | bytes 49160 | tf_op jit(solution)/shard_map/ppermute | solution.py:13
  61.3 11.5 %collective-permute-start.2 = (bf16[1,1,8,8,128]{4,3,2,1,0:T(8,128)(2,1)S(1)}, bf16[1,1,8,8,128]{4,3,2,1,0:T(8,128)(2,1)S(1)}, u32[]{:S(2)}, u32[]{:S(2)}) collective-permute-start(bf16[1,1,8,8,128]{4,3,2,1,0:T(8,128)(2,1)S(1)} %get-tuple-element.122), channel_id=1, source_target_pairs={{0,16},{16,32},{32,48},{1,17},{17,33},{33,49},{2,18},{18,34},{34,5... | collective-permute-start | bytes 49160 | tf_op jit(solution)/shard_map/ppermute | solution.py:12
  64.7 8.1 %collective-permute-start.3 = (bf16[1,1,8,8,128]{4,3,2,1,0:T(8,128)(2,1)S(1)}, bf16[1,1,8,8,128]{4,3,2,1,0:T(8,128)(2,1)S(1)}, u32[]{:S(2)}, u32[]{:S(2)}) collective-permute-start(bf16[1,1,8,8,128]{4,3,2,1,0:T(8,128)(2,1)S(1)} %get-tuple-element.121), channel_id=1, source_target_pairs={{16,0},{32,16},{48,32},{17,1},{33,17},{49,33},{18,2},{34,18},{50,3... | collective-permute-start | bytes 49160 | tf_op jit(solution)/shard_map/ppermute | solution.py:13
  71.4 2.4 %copy-start = (bf16[8,14,128,128]{3,2,1,0:T(8,128)(2,1)S(1)}, bf16[8,14,128,128]{3,2,1,0:T(8,128)(2,1)}, u32[]{:S(2)}) copy-start(bf16[8,14,128,128]{3,2,1,0:T(8,128)(2,1)} %all-gather.2.cloned.1.call-done) | copy-start | bytes 11010052
  76.9 13.1 %collective-permute-start.4 = (bf16[1,8,1,8,128]{4,3,2,1,0:T(8,128)(2,1)S(1)}, bf16[1,8,1,8,128]{4,3,2,1,0:T(8,128)(2,1)S(1)}, u32[]{:S(2)}, u32[]{:S(2)}) collective-permute-start(bf16[1,8,1,8,128]{4,3,2,1,0:T(8,128)(2,1)S(1)} %get-tuple-element.115), channel_id=1, source_target_pairs={{0,1},{1,2},{2,3},{3,4},{4,5},{5,6},{6,7},{7,8},{8,9},{9,10},{10,1... | collective-permute-start | bytes 49160 | tf_op jit(solution)/shard_map/ppermute | solution.py:12
  79.2 10.8 %collective-permute-start.5 = (bf16[1,8,1,8,128]{4,3,2,1,0:T(8,128)(2,1)S(1)}, bf16[1,8,1,8,128]{4,3,2,1,0:T(8,128)(2,1)S(1)}, u32[]{:S(2)}, u32[]{:S(2)}) collective-permute-start(bf16[1,8,1,8,128]{4,3,2,1,0:T(8,128)(2,1)S(1)} %get-tuple-element.116), channel_id=1, source_target_pairs={{1,0},{2,1},{3,2},{4,3},{5,4},{6,5},{7,6},{8,7},{9,8},{10,9},{11,1... | collective-permute-start | bytes 49160 | tf_op jit(solution)/shard_map/ppermute | solution.py:13
  84.0 6.5 %collective-permute-start.6 = (bf16[1,1,8,8,128]{4,3,2,1,0:T(8,128)(2,1)S(1)}, bf16[1,1,8,8,128]{4,3,2,1,0:T(8,128)(2,1)S(1)}, u32[]{:S(2)}, u32[]{:S(2)}) collective-permute-start(bf16[1,1,8,8,128]{4,3,2,1,0:T(8,128)(2,1)S(1)} %get-tuple-element.114), channel_id=1, source_target_pairs={{0,16},{16,32},{32,48},{1,17},{17,33},{33,49},{2,18},{18,34},{34,5... | collective-permute-start | bytes 49160 | tf_op jit(solution)/shard_map/ppermute | solution.py:12
  88.5 5.6 %collective-permute-start.7 = (bf16[1,1,8,8,128]{4,3,2,1,0:T(8,128)(2,1)S(1)}, bf16[1,1,8,8,128]{4,3,2,1,0:T(8,128)(2,1)S(1)}, u32[]{:S(2)}, u32[]{:S(2)}) collective-permute-start(bf16[1,1,8,8,128]{4,3,2,1,0:T(8,128)(2,1)S(1)} %get-tuple-element.113), channel_id=1, source_target_pairs={{16,0},{32,16},{48,32},{17,1},{33,17},{49,33},{18,2},{34,18},{50,3... | collective-permute-start | bytes 49160 | tf_op jit(solution)/shard_map/ppermute | solution.py:13
  96.6 13.6 %collective-permute-start.10 = (bf16[1,1,8,8,128]{4,3,2,1,0:T(8,128)(2,1)S(1)}, bf16[1,1,8,8,128]{4,3,2,1,0:T(8,128)(2,1)S(1)}, u32[]{:S(2)}, u32[]{:S(2)}) collective-permute-start(bf16[1,1,8,8,128]{4,3,2,1,0:T(8,128)(2,1)S(1)} %get-tuple-element.106), channel_id=1, source_target_pairs={{0,16},{16,32},{32,48},{1,17},{17,33},{33,49},{2,18},{18,34},{34,5... | collective-permute-start | bytes 49160 | tf_op jit(solution)/shard_map/ppermute | solution.py:12
  100.0 10.2 %collective-permute-start.11 = (bf16[1,1,8,8,128]{4,3,2,1,0:T(8,128)(2,1)S(1)}, bf16[1,1,8,8,128]{4,3,2,1,0:T(8,128)(2,1)S(1)}, u32[]{:S(2)}, u32[]{:S(2)}) collective-permute-start(bf16[1,1,8,8,128]{4,3,2,1,0:T(8,128)(2,1)S(1)} %get-tuple-element.105), channel_id=1, source_target_pairs={{16,0},{32,16},{48,32},{17,1},{33,17},{49,33},{18,2},{34,18},{50,3... | collective-permute-start | bytes 49160 | tf_op jit(solution)/shard_map/ppermute | solution.py:13
  101.3 7.2 %collective-permute-start.8 = (bf16[1,8,1,8,128]{4,3,2,1,0:T(8,128)(2,1)S(1)}, bf16[1,8,1,8,128]{4,3,2,1,0:T(8,128)(2,1)S(1)}, u32[]{:S(2)}, u32[]{:S(2)}) collective-permute-start(bf16[1,8,1,8,128]{4,3,2,1,0:T(8,128)(2,1)S(1)} %get-tuple-element.107), channel_id=1, source_target_pairs={{0,1},{1,2},{2,3},{3,4},{4,5},{5,6},{6,7},{7,8},{8,9},{9,10},{10,1... | collective-permute-start | bytes 49160 | tf_op jit(solution)/shard_map/ppermute | solution.py:12
  103.2 6.6 %collective-permute-start.9 = (bf16[1,8,1,8,128]{4,3,2,1,0:T(8,128)(2,1)S(1)}, bf16[1,8,1,8,128]{4,3,2,1,0:T(8,128)(2,1)S(1)}, u32[]{:S(2)}, u32[]{:S(2)}) collective-permute-start(bf16[1,8,1,8,128]{4,3,2,1,0:T(8,128)(2,1)S(1)} %get-tuple-element.108), channel_id=1, source_target_pairs={{1,0},{2,1},{3,2},{4,3},{5,4},{6,5},{7,6},{8,7},{9,8},{10,9},{11,1... | collective-permute-start | bytes 49160 | tf_op jit(solution)/shard_map/ppermute | solution.py:13
  112.7 13.4 %collective-permute-start.12 = (bf16[1,8,1,8,128]{4,3,2,1,0:T(8,128)(2,1)S(1)}, bf16[1,8,1,8,128]{4,3,2,1,0:T(8,128)(2,1)S(1)}, u32[]{:S(2)}, u32[]{:S(2)}) collective-permute-start(bf16[1,8,1,8,128]{4,3,2,1,0:T(8,128)(2,1)S(1)} %get-tuple-element.99), channel_id=1, source_target_pairs={{0,1},{1,2},{2,3},{3,4},{4,5},{5,6},{6,7},{7,8},{8,9},{9,10},{10,1... | collective-permute-start | bytes 49160 | tf_op jit(solution)/shard_map/ppermute | solution.py:12
  115.8 10.2 %collective-permute-start.13 = (bf16[1,8,1,8,128]{4,3,2,1,0:T(8,128)(2,1)S(1)}, bf16[1,8,1,8,128]{4,3,2,1,0:T(8,128)(2,1)S(1)}, u32[]{:S(2)}, u32[]{:S(2)}) collective-permute-start(bf16[1,8,1,8,128]{4,3,2,1,0:T(8,128)(2,1)S(1)} %get-tuple-element.100), channel_id=1, source_target_pairs={{1,0},{2,1},{3,2},{4,3},{5,4},{6,5},{7,6},{8,7},{9,8},{10,9},{11,1... | collective-permute-start | bytes 49160 | tf_op jit(solution)/shard_map/ppermute | solution.py:13
  120.0 6.5 %collective-permute-start.14 = (bf16[1,1,8,8,128]{4,3,2,1,0:T(8,128)(2,1)S(1)}, bf16[1,1,8,8,128]{4,3,2,1,0:T(8,128)(2,1)S(1)}, u32[]{:S(2)}, u32[]{:S(2)}) collective-permute-start(bf16[1,1,8,8,128]{4,3,2,1,0:T(8,128)(2,1)S(1)} %get-tuple-element.98), channel_id=1, source_target_pairs={{0,16},{16,32},{32,48},{1,17},{17,33},{33,49},{2,18},{18,34},{34,5... | collective-permute-start | bytes 49160 | tf_op jit(solution)/shard_map/ppermute | solution.py:12
  124.6 5.6 %collective-permute-start.15 = (bf16[1,1,8,8,128]{4,3,2,1,0:T(8,128)(2,1)S(1)}, bf16[1,1,8,8,128]{4,3,2,1,0:T(8,128)(2,1)S(1)}, u32[]{:S(2)}, u32[]{:S(2)}) collective-permute-start(bf16[1,1,8,8,128]{4,3,2,1,0:T(8,128)(2,1)S(1)} %get-tuple-element.97), channel_id=1, source_target_pairs={{16,0},{32,16},{48,32},{17,1},{33,17},{49,33},{18,2},{34,18},{50,3... | collective-permute-start | bytes 49160 | tf_op jit(solution)/shard_map/ppermute | solution.py:13
  132.6 11.6 %collective-permute-start.16 = (bf16[1,8,1,8,128]{4,3,2,1,0:T(8,128)(2,1)S(1)}, bf16[1,8,1,8,128]{4,3,2,1,0:T(8,128)(2,1)S(1)}, u32[]{:S(2)}, u32[]{:S(2)}) collective-permute-start(bf16[1,8,1,8,128]{4,3,2,1,0:T(8,128)(2,1)S(1)} %get-tuple-element.91), channel_id=1, source_target_pairs={{0,1},{1,2},{2,3},{3,4},{4,5},{5,6},{6,7},{7,8},{8,9},{9,10},{10,1... | collective-permute-start | bytes 49160 | tf_op jit(solution)/shard_map/ppermute | solution.py:12
  135.5 8.8 %collective-permute-start.17 = (bf16[1,8,1,8,128]{4,3,2,1,0:T(8,128)(2,1)S(1)}, bf16[1,8,1,8,128]{4,3,2,1,0:T(8,128)(2,1)S(1)}, u32[]{:S(2)}, u32[]{:S(2)}) collective-permute-start(bf16[1,8,1,8,128]{4,3,2,1,0:T(8,128)(2,1)S(1)} %get-tuple-element.92), channel_id=1, source_target_pairs={{1,0},{2,1},{3,2},{4,3},{5,4},{6,5},{7,6},{8,7},{9,8},{10,9},{11,1... | collective-permute-start | bytes 49160 | tf_op jit(solution)/shard_map/ppermute | solution.py:13
  139.7 5.0 %collective-permute-start.18 = (bf16[1,1,8,8,128]{4,3,2,1,0:T(8,128)(2,1)S(1)}, bf16[1,1,8,8,128]{4,3,2,1,0:T(8,128)(2,1)S(1)}, u32[]{:S(2)}, u32[]{:S(2)}) collective-permute-start(bf16[1,1,8,8,128]{4,3,2,1,0:T(8,128)(2,1)S(1)} %get-tuple-element.90), channel_id=1, source_target_pairs={{0,16},{16,32},{32,48},{1,17},{17,33},{33,49},{2,18},{18,34},{34,5... | collective-permute-start | bytes 49160 | tf_op jit(solution)/shard_map/ppermute | solution.py:12
  142.8 5.6 %collective-permute-start.19 = (bf16[1,1,8,8,128]{4,3,2,1,0:T(8,128)(2,1)S(1)}, bf16[1,1,8,8,128]{4,3,2,1,0:T(8,128)(2,1)S(1)}, u32[]{:S(2)}, u32[]{:S(2)}) collective-permute-start(bf16[1,1,8,8,128]{4,3,2,1,0:T(8,128)(2,1)S(1)} %get-tuple-element.89), channel_id=1, source_target_pairs={{16,0},{32,16},{48,32},{17,1},{33,17},{49,33},{18,2},{34,18},{50,3... | collective-permute-start | bytes 49160 | tf_op jit(solution)/shard_map/ppermute | solution.py:13
  150.8 10.5 %collective-permute-start.20 = (bf16[1,8,1,8,128]{4,3,2,1,0:T(8,128)(2,1)S(1)}, bf16[1,8,1,8,128]{4,3,2,1,0:T(8,128)(2,1)S(1)}, u32[]{:S(2)}, u32[]{:S(2)}) collective-permute-start(bf16[1,8,1,8,128]{4,3,2,1,0:T(8,128)(2,1)S(1)} %get-tuple-element.83), channel_id=1, source_target_pairs={{0,1},{1,2},{2,3},{3,4},{4,5},{5,6},{6,7},{7,8},{8,9},{9,10},{10,1... | collective-permute-start | bytes 49160 | tf_op jit(solution)/shard_map/ppermute | solution.py:12
  153.8 7.6 %collective-permute-start.21 = (bf16[1,8,1,8,128]{4,3,2,1,0:T(8,128)(2,1)S(1)}, bf16[1,8,1,8,128]{4,3,2,1,0:T(8,128)(2,1)S(1)}, u32[]{:S(2)}, u32[]{:S(2)}) collective-permute-start(bf16[1,8,1,8,128]{4,3,2,1,0:T(8,128)(2,1)S(1)} %get-tuple-element.84), channel_id=1, source_target_pairs={{1,0},{2,1},{3,2},{4,3},{5,4},{6,5},{7,6},{8,7},{9,8},{10,9},{11,1... | collective-permute-start | bytes 49160 | tf_op jit(solution)/shard_map/ppermute | solution.py:13
  157.9 3.9 %collective-permute-start.22 = (bf16[1,1,8,8,128]{4,3,2,1,0:T(8,128)(2,1)S(1)}, bf16[1,1,8,8,128]{4,3,2,1,0:T(8,128)(2,1)S(1)}, u32[]{:S(2)}, u32[]{:S(2)}) collective-permute-start(bf16[1,1,8,8,128]{4,3,2,1,0:T(8,128)(2,1)S(1)} %get-tuple-element.82), channel_id=1, source_target_pairs={{0,16},{16,32},{32,48},{1,17},{17,33},{33,49},{2,18},{18,34},{34,5... | collective-permute-start | bytes 49160 | tf_op jit(solution)/shard_map/ppermute | solution.py:12
  159.8 5.6 %collective-permute-start.23 = (bf16[1,1,8,8,128]{4,3,2,1,0:T(8,128)(2,1)S(1)}, bf16[1,1,8,8,128]{4,3,2,1,0:T(8,128)(2,1)S(1)}, u32[]{:S(2)}, u32[]{:S(2)}) collective-permute-start(bf16[1,1,8,8,128]{4,3,2,1,0:T(8,128)(2,1)S(1)} %get-tuple-element.81), channel_id=1, source_target_pairs={{16,0},{32,16},{48,32},{17,1},{33,17},{49,33},{18,2},{34,18},{50,3... | collective-permute-start | bytes 49160 | tf_op jit(solution)/shard_map/ppermute | solution.py:13
  167.9 10.7 %collective-permute-start.24 = (bf16[1,8,1,8,128]{4,3,2,1,0:T(8,128)(2,1)S(1)}, bf16[1,8,1,8,128]{4,3,2,1,0:T(8,128)(2,1)S(1)}, u32[]{:S(2)}, u32[]{:S(2)}) collective-permute-start(bf16[1,8,1,8,128]{4,3,2,1,0:T(8,128)(2,1)S(1)} %get-tuple-element.75), channel_id=1, source_target_pairs={{0,1},{1,2},{2,3},{3,4},{4,5},{5,6},{6,7},{7,8},{8,9},{9,10},{10,1... | collective-permute-start | bytes 49160 | tf_op jit(solution)/shard_map/ppermute | solution.py:12
  169.8 8.7 %collective-permute-start.25 = (bf16[1,8,1,8,128]{4,3,2,1,0:T(8,128)(2,1)S(1)}, bf16[1,8,1,8,128]{4,3,2,1,0:T(8,128)(2,1)S(1)}, u32[]{:S(2)}, u32[]{:S(2)}) collective-permute-start(bf16[1,8,1,8,128]{4,3,2,1,0:T(8,128)(2,1)S(1)} %get-tuple-element.76), channel_id=1, source_target_pairs={{1,0},{2,1},{3,2},{4,3},{5,4},{6,5},{7,6},{8,7},{9,8},{10,9},{11,1... | collective-permute-start | bytes 49160 | tf_op jit(solution)/shard_map/ppermute | solution.py:13
  175.0 4.0 %collective-permute-start.26 = (bf16[1,1,8,8,128]{4,3,2,1,0:T(8,128)(2,1)S(1)}, bf16[1,1,8,8,128]{4,3,2,1,0:T(8,128)(2,1)S(1)}, u32[]{:S(2)}, u32[]{:S(2)}) collective-permute-start(bf16[1,1,8,8,128]{4,3,2,1,0:T(8,128)(2,1)S(1)} %get-tuple-element.74), channel_id=1, source_target_pairs={{0,16},{16,32},{32,48},{1,17},{17,33},{33,49},{2,18},{18,34},{34,5... | collective-permute-start | bytes 49160 | tf_op jit(solution)/shard_map/ppermute | solution.py:12
  176.9 5.6 %collective-permute-start.27 = (bf16[1,1,8,8,128]{4,3,2,1,0:T(8,128)(2,1)S(1)}, bf16[1,1,8,8,128]{4,3,2,1,0:T(8,128)(2,1)S(1)}, u32[]{:S(2)}, u32[]{:S(2)}) collective-permute-start(bf16[1,1,8,8,128]{4,3,2,1,0:T(8,128)(2,1)S(1)} %get-tuple-element.73), channel_id=1, source_target_pairs={{16,0},{32,16},{48,32},{17,1},{33,17},{49,33},{18,2},{34,18},{50,3... | collective-permute-start | bytes 49160 | tf_op jit(solution)/shard_map/ppermute | solution.py:13
  185.0 10.5 %collective-permute-start.28 = (bf16[1,8,1,8,128]{4,3,2,1,0:T(8,128)(2,1)S(1)}, bf16[1,8,1,8,128]{4,3,2,1,0:T(8,128)(2,1)S(1)}, u32[]{:S(2)}, u32[]{:S(2)}) collective-permute-start(bf16[1,8,1,8,128]{4,3,2,1,0:T(8,128)(2,1)S(1)} %get-tuple-element.67), channel_id=1, source_target_pairs={{0,1},{1,2},{2,3},{3,4},{4,5},{5,6},{6,7},{7,8},{8,9},{9,10},{10,1... | collective-permute-start | bytes 49160 | tf_op jit(solution)/shard_map/ppermute | solution.py:12
  186.9 8.6 %collective-permute-start.29 = (bf16[1,8,1,8,128]{4,3,2,1,0:T(8,128)(2,1)S(1)}, bf16[1,8,1,8,128]{4,3,2,1,0:T(8,128)(2,1)S(1)}, u32[]{:S(2)}, u32[]{:S(2)}) collective-permute-start(bf16[1,8,1,8,128]{4,3,2,1,0:T(8,128)(2,1)S(1)} %get-tuple-element.68), channel_id=1, source_target_pairs={{1,0},{2,1},{3,2},{4,3},{5,4},{6,5},{7,6},{8,7},{9,8},{10,9},{11,1... | collective-permute-start | bytes 49160 | tf_op jit(solution)/shard_map/ppermute | solution.py:13
  192.0 3.9 %collective-permute-start.30 = (bf16[1,1,8,8,128]{4,3,2,1,0:T(8,128)(2,1)S(1)}, bf16[1,1,8,8,128]{4,3,2,1,0:T(8,128)(2,1)S(1)}, u32[]{:S(2)}, u32[]{:S(2)}) collective-permute-start(bf16[1,1,8,8,128]{4,3,2,1,0:T(8,128)(2,1)S(1)} %get-tuple-element.66), channel_id=1, source_target_pairs={{0,16},{16,32},{32,48},{1,17},{17,33},{33,49},{2,18},{18,34},{34,5... | collective-permute-start | bytes 49160 | tf_op jit(solution)/shard_map/ppermute | solution.py:12
  194.0 5.6 %collective-permute-start.31 = (bf16[1,1,8,8,128]{4,3,2,1,0:T(8,128)(2,1)S(1)}, bf16[1,1,8,8,128]{4,3,2,1,0:T(8,128)(2,1)S(1)}, u32[]{:S(2)}, u32[]{:S(2)}) collective-permute-start(bf16[1,1,8,8,128]{4,3,2,1,0:T(8,128)(2,1)S(1)} %get-tuple-element.65), channel_id=1, source_target_pairs={{16,0},{32,16},{48,32},{17,1},{33,17},{49,33},{18,2},{34,18},{50,3... | collective-permute-start | bytes 49160 | tf_op jit(solution)/shard_map/ppermute | solution.py:13
Sparse Core Ops, SparseCore 0:
  9.5 40.5 all-gather.1
